TPU v7x, 256 devices: a whole 4x4x8 slice. The times are simulated.
256 devices in a mesh: shard: 64 (over y, z_hi, x), rep: 4 (over z_lo, core).
Axes of the slice: x: 4, y: 4, z: 8 (z_hi: 4, z_lo: 2; z = z_hi * 2 + z_lo), core: 2. Of those that a mesh axis runs over, the one named last changes fastest.
Arguments:
- rows_in: bfloat16 [131072, 2048], P(('shard', 'rep')), may hold values from -24 to 24
- cotangent: bfloat16 [131072, 2048], P(('shard', 'rep')), may hold values from -24 to 24
- expert_counts: int32 [256, 2], P(('shard', 'rep')), may hold values from 0 to 512, as said below
- weights: bfloat16 [2048, 2, 1152], P('shard'), may hold values from -0.125 to 0.125
Outputs:
- rows_out: bfloat16 [131072, 2048], P(('shard', 'rep'))
- rows_grad: bfloat16 [131072, 2048], P(('shard', 'rep'))
- weight_grad: float32 [2048, 2, 1152], P('shard')
Inputs may be any that keep to these rules, and one draw needn't show every extreme that they name: `expert_counts`: on each device the experts' regions, each padded to a multiple of 128 rows, follow one another from row 0 and together fill at most 512 rows; some device fills all 512; one expert on some device holds all 512 rows.
All inputs are finite; a program needn't handle non-finite values.
Results may differ from a plain program's by a relative error of at most 0.0095.
Values may be sent and summed in bfloat16 or wider, within the bound.
No kernel may reach another device: no remote copies, remote signals or barrier semaphores. Data moves between devices by JAX's collectives and lax.ppermute only.
A program may use at most 128 MiB of HBM per device.

v0:
```python
import jax
import jax.numpy as jnp
from jax import lax
from jax.sharding import PartitionSpec as P

BLOCK = 128


def expert_block(inputs, upstream, expert_slab):
    hidden_width = expert_slab.shape[1] // 3
    gate_up = expert_slab[:, : 2 * hidden_width]
    down_t = expert_slab[:, 2 * hidden_width :]
    project = jnp.dot(inputs, gate_up, preferred_element_type=jnp.float32)
    gate_pre = project[:, :hidden_width]
    up_pre = project[:, hidden_width:]
    gate_sigmoid = jax.nn.sigmoid(gate_pre)
    active = gate_pre * gate_sigmoid
    hidden = (active * up_pre).astype(jnp.bfloat16)
    output = lax.dot_general(
        hidden, down_t, (((1,), (1,)), ((), ())), preferred_element_type=jnp.float32
    ).astype(jnp.bfloat16)
    hidden_grad = jnp.dot(upstream, down_t, preferred_element_type=jnp.float32)
    down_grad = lax.dot_general(
        upstream, hidden, (((0,), (0,)), ((), ())), preferred_element_type=jnp.float32
    )
    gate_grad = hidden_grad * up_pre * gate_sigmoid * (1.0 + gate_pre * (1.0 - gate_sigmoid))
    up_grad = hidden_grad * active
    joint_grad = jnp.concatenate([gate_grad, up_grad], axis=1).astype(jnp.bfloat16)
    proj_grad = lax.dot_general(
        inputs, joint_grad, (((0,), (0,)), ((), ())), preferred_element_type=jnp.float32
    )
    input_grad = lax.dot_general(
        joint_grad, gate_up, (((1,), (1,)), ((), ())), preferred_element_type=jnp.float32
    ).astype(jnp.bfloat16)
    return (output, input_grad, jnp.concatenate([proj_grad, down_grad], axis=1))


def alive_rows(counts, total_rows):
    padded = (counts + BLOCK - 1) // BLOCK * BLOCK
    starts = jnp.cumsum(padded) - padded
    position = jnp.arange(total_rows, dtype=jnp.int32)
    inside = (position[:, None] >= starts[None, :]) & (
        position[:, None] < (starts + counts)[None, :]
    )
    return (jnp.any(inside, axis=1), padded, starts)


def run_expert(expert_slab, inputs, upstream, start_row, nblocks, outputs, input_grads):

    def block_step(block_index, state):
        outputs, input_grads, grad_total = state
        row_begin = start_row + block_index * BLOCK
        block_in = lax.dynamic_slice_in_dim(inputs, row_begin, BLOCK, 0)
        block_up = lax.dynamic_slice_in_dim(upstream, row_begin, BLOCK, 0)
        output, input_grad, grad_piece = expert_block(block_in, block_up, expert_slab)
        outputs = lax.dynamic_update_slice_in_dim(outputs, output, row_begin, 0)
        input_grads = lax.dynamic_update_slice_in_dim(input_grads, input_grad, row_begin, 0)
        return (outputs, input_grads, grad_total + grad_piece)

    start_grad = jnp.zeros(expert_slab.shape, jnp.float32)
    return lax.fori_loop(jnp.int32(0), nblocks, block_step, (outputs, input_grads, start_grad))


def reduce_grads(grads):
    partial_sum = lax.psum_scatter(grads, "shard", scatter_dimension=0, tiled=True)
    return lax.psum(partial_sum.astype(jnp.bfloat16), "rep").astype(jnp.float32)


def local(rows_in, cotangent, expert_counts, weights):
    counts = expert_counts[0]
    alive, padded, starts = alive_rows(counts, rows_in.shape[0])
    inputs = jnp.where(alive[:, None], rows_in, jnp.zeros_like(rows_in))
    upstream = jnp.where(alive[:, None], cotangent, jnp.zeros_like(cotangent))
    outputs = jnp.zeros_like(rows_in)
    input_grads = jnp.zeros_like(rows_in)
    experts = weights.shape[1]
    pieces = []
    gathered = lax.all_gather(weights, "shard", axis=0, tiled=True)
    for expert in range(experts):
        outputs, input_grads, grad_total = run_expert(
            gathered[:, expert],
            inputs,
            upstream,
            starts[expert],
            padded[expert] // BLOCK,
            outputs,
            input_grads,
        )
        pieces.append(grad_total)
    reduced = reduce_grads(jnp.stack(pieces, axis=1))
    return (outputs, input_grads, reduced)


def solution(mesh):
    in_specs = (
        P(("shard", "rep"), None),
        P(("shard", "rep"), None),
        P(("shard", "rep"), None),
        P("shard", None, None),
    )
    out_specs = (P(("shard", "rep"), None), P(("shard", "rep"), None), P("shard", None, None))
    return jax.shard_map(local, mesh=mesh, in_specs=in_specs, out_specs=out_specs, check_vma=False)
```

profile of v0, /device:TPU:1, one launch (start us, length us, event | category | flops | bytes accessed | tf_op | source)
XLA Modules:
  0.0 622.5 jit_solution(16797978285030678725)
XLA Ops:
  7.2 1.6 copy.14
  17.0 4.0 broadcast_select_fusion
  21.0 109.1 %all-gather.2.cloned.1.call-done = bf16[2048,2,1152]{2,0,1:T(8,128)(2,1)} async-done(((bf16[32,2,1152]{2,0,1:T(8,128)(2,1)}), bf16[2048,2,1152]{2,0,1:T(8,128)(2,1)}) %all-gather.2.cloned.1.call-update) | async-done | bytes 9437200 | tf_op jit(solution)/shard_map/all_gather | solution.py:78
  130.1 8.2 %slice_bitcast_fusion = (bf16[2048,1152]{1,0:T(8,128)(2,1)}, bf16[2048,1152]{1,0:T(8,128)(2,1)}) fusion(bf16[2048,2,1152]{2,0,1:T(8,128)(2,1)} %all-gather.2.cloned.1.call-done), kind=kLoop, calls=%fused_computation.57 | loop fusion | bytes 18874368 | tf_op jit(solution)/shard_map/squeeze | solution.py:81
  138.3 1.6 broadcast.130.clone
  139.8 1.6 broadcast.130
  141.4 4.8 broadcast.131.clone
  146.2 97.8 %while.28 = (s32[]{:T(128)}, bf16[512,2048]{1,0:T(8,128)(2,1)}, bf16[512,2048]{1,0:T(8,128)(2,1)}, f32[2048,1152]{0,1:T(8,128)}, s32[]{:T(128)}, /*index=5*/s32[...) while((s32[]{:T(128)}, bf16[512,2048]{1,0:T(8,128)(2,1)}, ...), condition=%wide.region_3.4_spmd, body=%wide.region_2.3_spmd.sunk | while | flops 1818705920 | bytes 72974568 | solution.py:61
  146.9 2.6 fusion.87
  150.2 1.5 multiply_convert_fusion.8
  152.3 1.1 fusion.88
  153.5 3.8 dynamic_update_slice.17
  157.3 3.8 dynamic_update_slice.16
  161.1 1.7 fusion.89
  162.7 1.0 fusion.90
  163.8 7.1 %maximum_add_fusion.4 = f32[2048,1152]{0,1:T(8,128)} fusion(f32[2048,1152]{0,1:T(8,128)} %get-tuple-element.311, f32[2048,384]{0,1:T(8,128)S(1)} %fusion.89, f32[2048,768]{0,1:T(8,128)S(1)} %fusion.90), kind=kLoop, calls=%fused_computation.clone.1 | loop fusion | flops 4718592 | bytes 28311552 | tf_op jit(solution)/shard_map/while/body/add | solution.py:58
  171.6 2.6 fusion.87
  174.8 1.5 multiply_convert_fusion.8
  177.0 1.2 fusion.88
  178.1 3.8 dynamic_update_slice.17
  182.0 3.8 dynamic_update_slice.16
  185.8 1.7 fusion.89
  187.4 1.0 fusion.90
  188.5 7.1 %maximum_add_fusion.4 = f32[2048,1152]{0,1:T(8,128)} fusion(f32[2048,1152]{0,1:T(8,128)} %get-tuple-element.311, f32[2048,384]{0,1:T(8,128)S(1)} %fusion.89, f32[2048,768]{0,1:T(8,128)S(1)} %fusion.90), kind=kLoop, calls=%fused_computation.clone.1 | loop fusion | flops 4718592 | bytes 28311552 | tf_op jit(solution)/shard_map/while/body/add | solution.py:58
  196.3 2.6 fusion.87
  199.5 1.5 multiply_convert_fusion.8
  201.7 1.2 fusion.88
  202.8 3.8 dynamic_update_slice.17
  206.6 3.8 dynamic_update_slice.16
  210.4 1.7 fusion.89
  212.1 1.0 fusion.90
  213.1 7.1 %maximum_add_fusion.4 = f32[2048,1152]{0,1:T(8,128)} fusion(f32[2048,1152]{0,1:T(8,128)} %get-tuple-element.311, f32[2048,384]{0,1:T(8,128)S(1)} %fusion.89, f32[2048,768]{0,1:T(8,128)S(1)} %fusion.90), kind=kLoop, calls=%fused_computation.clone.1 | loop fusion | flops 4718592 | bytes 28311552 | tf_op jit(solution)/shard_map/while/body/add | solution.py:58
  220.9 2.6 fusion.87
  224.2 1.5 multiply_convert_fusion.8
  226.3 1.2 fusion.88
  227.5 3.3 dynamic_update_slice.17
  230.8 3.3 dynamic_update_slice.16
  234.2 1.7 fusion.89
  235.8 1.0 fusion.90
  236.9 7.1 %maximum_add_fusion.4 = f32[2048,1152]{0,1:T(8,128)} fusion(f32[2048,1152]{0,1:T(8,128)} %get-tuple-element.311, f32[2048,384]{0,1:T(8,128)S(1)} %fusion.89, f32[2048,768]{0,1:T(8,128)S(1)} %fusion.90), kind=kLoop, calls=%fused_computation.clone.1 | loop fusion | flops 4718592 | bytes 28311552 | tf_op jit(solution)/shard_map/while/body/add | solution.py:58
  244.0 9.6 %copy.15 = f32[2048,1152]{1,0:T(8,128)} copy(f32[2048,1152]{0,1:T(8,128)} %get-tuple-element.107) | data formatting | bytes 18874368 | tf_op jit(solution)/shard_map/while | solution.py:61
  253.6 4.8 broadcast.131
  258.5 9.7 %copy.16 = f32[2048,1152]{1,0:T(8,128)} copy(f32[2048,1152]{0,1:T(8,128)} %get-tuple-element.108) | data formatting | bytes 18874368 | tf_op jit(solution)/shard_map/while | solution.py:61
  268.2 14.5 %pad_maximum_fusion.6 = f32[2048,2,1152]{2,0,1:T(8,128)} fusion(f32[2048,1,1152]{2,0,1:T(8,128)} %bitcast.52, f32[2048,1,1152]{2,0,1:T(8,128)} %bitcast.51), kind=kLoop, calls=%fused_computation.56 | loop fusion | flops 4718592 | bytes 37748736 | tf_op jit(solution)/shard_map/stack | solution.py:90
  282.7 288.9 %reduce-scatter.2.cloned.1.call-done = f32[32,2,1152]{2,0,1:T(8,128)} async-done(((f32[2048,2,1152]{2,0,1:T(8,128)}), f32[32,2,1152]{2,0,1:T(8,128)}) %reduce-scatter.2.cloned.1.call-update) | async-done | bytes 294928 | tf_op jit(solution)/shard_map/reduce_scatter | solution.py:65
  571.6 1.6 convert_element_type.26
  573.3 40.9 %all-reduce.2.cloned.1.call-done = bf16[32,2,1152]{2,0,1:T(8,128)(2,1)} async-done(((bf16[32,2,1152]{2,0,1:T(8,128)(2,1)}), bf16[32,2,1152]{2,0,1:T(8,128)(2,1)}) %all-reduce.2.cloned.1.call-update) | async-done | bytes 147472 | tf_op jit(solution)/shard_map/psum | solution.py:66
  614.2 1.7 copy.17
  (25 shorter events, 8.1 us)
Async XLA Ops:
  7.2 122.9 %all-gather.2.cloned.1.call-start = ((), (), s32[]{:S(2)}) async-start(), calls=%async_computation.1 | async-start | bytes 9584640 | tf_op jit(solution)/shard_map/all_gather | solution.py:78
  8.8 562.8 %reduce-scatter.2.cloned.1.call-start = ((), (), s32[]{:S(2)}) async-start(), calls=%async_computation.2 | async-start | bytes 19169280 | tf_op jit(solution)/shard_map/reduce_scatter | solution.py:65
  146.9 3.3 copy-start.1
  171.6 3.3 copy-start.1
  196.2 3.3 copy-start.1
  220.9 3.3 copy-start.1
  282.7 331.6 %all-reduce.2.cloned.1.call-start = ((), (), s32[]{:S(2)}) async-start(), calls=%async_computation.3 | async-start | bytes 294912 | tf_op jit(solution)/shard_map/psum | solution.py:66
Sparse Core Ops, SparseCore 0:
  11.8 118.2 all-gather.1
  282.8 288.7 reduce-scatter.1
  575.0 39.1 all-reduce.1
where the time goes:
time: 624 us; the launch traced here: 623 us
  waiting for transfers between devices  439 us (70%)
  local copies, waits for them, and re-layouts  76.3 us (12%)
  other arithmetic  51 us (8%)
  matrix products  34.4 us (6%)
  between operations  19 us (3%)
    reduce_scatter x1, waiting for transfers between devices, reduce_grads(): lax.psum_scatter(grads, 'shard', scatter_dimension=0, tiled=True)  289 us
    all_gather x1, waiting for transfers between devices, local(): gathered = lax.all_gather(weights, 'shard', axis=0, tiled=True)  109 us
    psum x1, waiting for transfers between devices, reduce_grads(): return lax.psum(partial_sum.astype(jnp.bfloat16), 'rep').astype(jnp.float32)  40.9 us
    add x4, other arithmetic, block_step(): return (outputs, input_grads, grad_total + grad_piece)  28.6 us
    while x2, local copies, waits for them, and re-layouts, run_expert(): lax.fori_loop(jnp.int32(0), nblocks, block_step, (outputs, input_grads, s...  19.3 us
    dynamic_update_slice x4, local copies, waits for them, and re-layouts, block_step(): lax.dynamic_update_slice_in_dim(input_grads, input_grad, row_begin, 0)  14.8 us
    dynamic_update_slice x4, local copies, waits for them, and re-layouts, block_step(): outputs = lax.dynamic_update_slice_in_dim(outputs, output, row_begin, 0)  14.7 us
    another operation x1, other arithmetic, local(): reduced = reduce_grads(jnp.stack(pieces, axis=1))  14.5 us
  transfers between devices with their start and end apart: 3, of which 3 were waited for; matrix products, arithmetic and copies ran while one was open for 1% of the time, Pallas kernels for 0%

commit v1 on v0

--- a/solution.py
+++ b/solution.py
@@ -61,33 +61,42 @@
     return lax.fori_loop(jnp.int32(0), nblocks, block_step, (outputs, input_grads, start_grad))
 
 
-def reduce_grads(grads):
-    partial_sum = lax.psum_scatter(grads, "shard", scatter_dimension=0, tiled=True)
-    return lax.psum(partial_sum.astype(jnp.bfloat16), "rep").astype(jnp.float32)
+def core_pairs(n):
+    return [(i, i ^ 1) for i in range(n)]
+
+
+def chip_pairs(n):
+    return [(i, i ^ 2) for i in range(n)]
 
 
 def local(rows_in, cotangent, expert_counts, weights):
+    nrep = lax.axis_size("rep")
+    core = lax.axis_index("rep") % 2
+    other = 1 - core
     counts = expert_counts[0]
     alive, padded, starts = alive_rows(counts, rows_in.shape[0])
     inputs = jnp.where(alive[:, None], rows_in, jnp.zeros_like(rows_in))
     upstream = jnp.where(alive[:, None], cotangent, jnp.zeros_like(cotangent))
     outputs = jnp.zeros_like(rows_in)
     input_grads = jnp.zeros_like(rows_in)
-    experts = weights.shape[1]
-    pieces = []
-    gathered = lax.all_gather(weights, "shard", axis=0, tiled=True)
-    for expert in range(experts):
-        outputs, input_grads, grad_total = run_expert(
-            gathered[:, expert],
-            inputs,
-            upstream,
-            starts[expert],
-            padded[expert] // BLOCK,
-            outputs,
-            input_grads,
-        )
-        pieces.append(grad_total)
-    reduced = reduce_grads(jnp.stack(pieces, axis=1))
+
+    mine_local = lax.dynamic_index_in_dim(weights, core, 1, keepdims=False)
+    mine = lax.all_gather(mine_local, "shard", axis=0, tiled=True)
+    theirs = lax.ppermute(mine, "rep", core_pairs(nrep))
+
+    outputs, input_grads, grad_mine = run_expert(
+        mine, inputs, upstream, starts[core], padded[core] // BLOCK, outputs, input_grads
+    )
+    outputs, input_grads, grad_theirs = run_expert(
+        theirs, inputs, upstream, starts[other], padded[other] // BLOCK, outputs, input_grads
+    )
+    grad_mine = grad_mine + lax.ppermute(grad_theirs, "rep", core_pairs(nrep))
+    part = lax.psum_scatter(grad_mine, "shard", scatter_dimension=0, tiled=True)
+    part = part + lax.ppermute(part, "rep", chip_pairs(nrep))
+    part_other = lax.ppermute(part, "rep", core_pairs(nrep))
+    first = jnp.where(core == 0, part, part_other)
+    second = jnp.where(core == 0, part_other, part)
+    reduced = jnp.stack([first, second], axis=1)
     return (outputs, input_grads, reduced)
 
 

time: 624 us -> 543 us (0.87)
  waiting for transfers between devices: 439 us -> 354 us
  matrix products: 34.4 us -> 49 us
  local copies, waits for them, and re-layouts: 76.3 us -> 64.9 us
    psum x1 -> x0, waiting for transfers between devices: 40.9 us -> none  [reduce_grads(): return lax.psum(partial_sum.astype(jnp.bfloat16), 'rep').astype(jnp.float32)]
    reduce_scatter x1, waiting for transfers between devices: 289 us -> 258 us  [local(): part = lax.psum_scatter(grad_mine, 'shard', scatter_dimension=0, tiled=True)]
    all_gather x1, waiting for transfers between devices: 109 us -> 85.9 us  [local(): mine = lax.all_gather(mine_local, 'shard', axis=0, tiled=True)]
    another operation x2 -> x3, other arithmetic: 14.6 us -> 0.22 us  [the longest x1 14.5 us: local(): reduced = reduce_grads(jnp.stack(pieces, axis=1))]
    add x0 -> x2, other arithmetic: none -> 11.9 us  [the longest x1 11 us: local(): grad_mine = grad_mine + lax.ppermute(grad_theirs, 'rep', core_pairs(nrep))]
    ppermute x0 -> x4, waiting for transfers between devices: none -> 10 us  [the longest x1 5.37 us: local(): grad_mine = grad_mine + lax.ppermute(grad_theirs, 'rep', core_pairs(nrep))]
    squeeze x1 -> x0, local copies, waits for them, and re-layouts: 8.16 us -> none  [local(): gathered[:, expert]]
    dot_general x4, matrix products: 4.6 us -> 12.1 us  [expert_block(): lax.dot_general(joint_grad, gate_up, (((1,), (1,)), ((), ())), preferred_...]
  transfers between devices with their start and end apart: 3 -> 6, of which waited for: 3 -> 5; matrix products, arithmetic and copies ran while one was open for 1% -> 5% of each run, Pallas kernels for 0% -> 0%
where the time goes in v1:
time: 543 us; the launch traced here: 541 us
  waiting for transfers between devices  354 us (65%)
  local copies, waits for them, and re-layouts  64.9 us (12%)
  matrix products  49 us (9%)
  other arithmetic  46.3 us (9%)
  between operations  19.3 us (4%)
    reduce_scatter x1, waiting for transfers between devices, local(): part = lax.psum_scatter(grad_mine, 'shard', scatter_dimension=0, tiled=True)  258 us
    all_gather x1, waiting for transfers between devices, local(): mine = lax.all_gather(mine_local, 'shard', axis=0, tiled=True)  85.9 us
    add x4, other arithmetic, block_step(): return (outputs, input_grads, grad_total + grad_piece)  28.1 us
    while x2, local copies, waits for them, and re-layouts, run_expert(): lax.fori_loop(jnp.int32(0), nblocks, block_step, (outputs, input_grads, s...  19.2 us
    dynamic_update_slice x4, local copies, waits for them, and re-layouts, block_step(): lax.dynamic_update_slice_in_dim(input_grads, input_grad, row_begin, 0)  14.8 us
    dynamic_update_slice x4, local copies, waits for them, and re-layouts, block_step(): outputs = lax.dynamic_update_slice_in_dim(outputs, output, row_begin, 0)  14.7 us
    another operation x4, local copies, waits for them, and re-layouts  12.9 us
    dot_general x4, matrix products, expert_block(): lax.dot_general(joint_grad, gate_up, (((1,), (1,)), ((), ())), preferred_...  12.1 us
  transfers between devices with their start and end apart: 6, of which 5 were waited for; matrix products, arithmetic and copies ran while one was open for 5% of the time, Pallas kernels for 0%

profile of v1, /device:TPU:1, one launch (start us, length us, event | category | flops | bytes accessed | tf_op | source)
XLA Modules:
  0.0 541.4 jit_solution(4028579359877416459)
XLA Ops:
  17.1 4.0 broadcast_select_fusion
  21.1 85.9 %all-gather.3.cloned.1.call-done = bf16[2048,1,1152]{2,0,1:T(8,128)(2,1)} async-done(((bf16[32,1,1152]{2,0,1:T(8,128)(2,1)}), bf16[2048,1,1152]{2,0,1:T(8,128)(2,1)}) %all-gather.3.cloned.1.call-update) | async-done | bytes 4718608 | tf_op jit(solution)/shard_map/all_gather | solution.py:84
  107.7 1.6 broadcast.131.clone
  109.3 1.6 broadcast.131
  110.9 4.9 broadcast.132.clone
  115.7 4.8 broadcast.132
  120.6 109.6 %while.29 = (s32[]{:T(128)}, bf16[512,2048]{1,0:T(8,128)(2,1)}, bf16[512,2048]{1,0:T(8,128)(2,1)}, f32[2048,1152]{0,1:T(8,128)}, s32[]{:T(128)}, /*index=5*/s32[...) while((s32[]{:T(128)}, bf16[512,2048]{1,0:T(8,128)(2,1)}, ...), condition=%wide.region_5.6_spmd, body=%wide.region_4.5_spmd.sunk | while | flops 1818705920 | bytes 54100176 | solution.py:61
  121.3 2.5 fusion.99
  123.8 2.0 multiply_convert_fusion.9
  125.8 2.0 convolution_convert_fusion.5
  127.9 3.0 fusion.100
  130.9 3.8 dynamic_update_slice.19
  134.7 3.8 dynamic_update_slice.18
  138.5 1.7 fusion.101
  140.2 1.0 fusion.102
  141.2 7.0 %maximum_add_fusion.5 = f32[2048,1152]{0,1:T(8,128)} fusion(f32[2048,1152]{0,1:T(8,128)} %get-tuple-element.350, f32[2048,384]{0,1:T(8,128)S(1)} %fusion.101, f32[2048,768]{0,1:T(8,128)S(1)} %fusion.102), kind=kLoop, calls=%fused_computation.28.clone.1 | loop fusion | flops 4718592 | bytes 28311552 | tf_op jit(solution)/shard_map/while/body/add | solution.py:58
  148.9 2.5 fusion.99
  151.4 2.0 multiply_convert_fusion.9
  153.5 2.0 convolution_convert_fusion.5
  155.5 3.0 fusion.100
  158.5 3.8 dynamic_update_slice.19
  162.4 3.8 dynamic_update_slice.18
  166.1 1.7 fusion.101
  167.8 1.0 fusion.102
  168.8 7.0 %maximum_add_fusion.5 = f32[2048,1152]{0,1:T(8,128)} fusion(f32[2048,1152]{0,1:T(8,128)} %get-tuple-element.350, f32[2048,384]{0,1:T(8,128)S(1)} %fusion.101, f32[2048,768]{0,1:T(8,128)S(1)} %fusion.102), kind=kLoop, calls=%fused_computation.28.clone.1 | loop fusion | flops 4718592 | bytes 28311552 | tf_op jit(solution)/shard_map/while/body/add | solution.py:58
  176.6 2.5 fusion.99
  179.1 2.0 multiply_convert_fusion.9
  181.1 2.0 convolution_convert_fusion.5
  183.1 3.0 fusion.100
  186.2 3.8 dynamic_update_slice.19
  190.0 3.8 dynamic_update_slice.18
  193.8 1.7 fusion.101
  196.5 7.0 %maximum_add_fusion.5 = f32[2048,1152]{0,1:T(8,128)} fusion(f32[2048,1152]{0,1:T(8,128)} %get-tuple-element.350, f32[2048,384]{0,1:T(8,128)S(1)} %fusion.101, f32[2048,768]{0,1:T(8,128)S(1)} %fusion.102), kind=kLoop, calls=%fused_computation.28.clone.1 | loop fusion | flops 4718592 | bytes 28311552 | tf_op jit(solution)/shard_map/while/body/add | solution.py:58
  204.2 2.5 fusion.99
  206.7 2.0 multiply_convert_fusion.9
  208.7 2.0 convolution_convert_fusion.5
  210.8 3.0 fusion.100
  213.8 3.3 dynamic_update_slice.19
  217.2 3.3 dynamic_update_slice.18
  220.5 1.7 fusion.101
  223.2 7.0 %maximum_add_fusion.5 = f32[2048,1152]{0,1:T(8,128)} fusion(f32[2048,1152]{0,1:T(8,128)} %get-tuple-element.350, f32[2048,384]{0,1:T(8,128)S(1)} %fusion.101, f32[2048,768]{0,1:T(8,128)S(1)} %fusion.102), kind=kLoop, calls=%fused_computation.28.clone.1 | loop fusion | flops 4718592 | bytes 28311552 | tf_op jit(solution)/shard_map/while/body/add | solution.py:58
  230.2 9.6 %copy.16 = f32[2048,1152]{1,0:T(8,128)} copy(f32[2048,1152]{0,1:T(8,128)} %get-tuple-element.108) | data formatting | bytes 18874368 | tf_op jit(solution)/shard_map/while | solution.py:61
  239.8 9.6 %copy.17 = f32[2048,1152]{1,0:T(8,128)} copy(f32[2048,1152]{0,1:T(8,128)} %get-tuple-element.107) | data formatting | bytes 18874368 | tf_op jit(solution)/shard_map/while | solution.py:61
  249.4 5.4 collective-permute-done.1
  254.8 11.0 %add.107 = f32[2048,1152]{1,0:T(8,128)} add(f32[2048,1152]{1,0:T(8,128)} %copy.17, f32[2048,1152]{1,0:T(8,128)} %collective-permute-done.1) | non-fusion elementwise | flops 2359296 | bytes 28311552 | tf_op jit(solution)/shard_map/add | solution.py:93
  265.8 257.7 %reduce-scatter.2.cloned.1.call-done = f32[32,1152]{1,0:T(8,128)} async-done(((f32[2048,1152]{1,0:T(8,128)}), f32[32,1152]{1,0:T(8,128)}) %reduce-scatter.2.cloned.1.call-update) | async-done | bytes 147472 | tf_op jit(solution)/shard_map/reduce_scatter | solution.py:94
  524.1 3.6 collective-permute-done.2
  528.7 3.9 collective-permute-start.3
  (28 shorter events, 11.0 us)
Async XLA Ops:
  7.2 0.9 copy-start
  7.2 99.8 %all-gather.3.cloned.1.call-start = ((), (), s32[]{:S(2)}) async-start(), calls=%async_computation.2 | async-start | bytes 4792320 | tf_op jit(solution)/shard_map/all_gather | solution.py:84
  8.9 514.6 %reduce-scatter.2.cloned.1.call-start = ((), (), s32[]{:S(2)}) async-start(), calls=%async_computation.1 | async-start | bytes 9584640 | tf_op jit(solution)/shard_map/reduce_scatter | solution.py:94
  107.0 8.7 %collective-permute-start = (bf16[2048,1152]{1,0:T(8,128)(2,1)}, bf16[2048,1152]{1,0:T(8,128)(2,1)}, u32[]{:S(2)}, u32[]{:S(2)}) collective-permute-start(bf16[2048,1152]{1,0:T(8,128)(2,1)} %bitcast.50), channel_id=1, source_target_pairs={{0,1},{1,0},{2,3},{3,2},{4,5},{5,4},{6,7},{7,6},{8,9},{9,8},{10,11... | collective-permute-start | bytes 14155784 | tf_op jit(solution)/shard_map/ppermute | solution.py:85
  239.8 15.0 %collective-permute-start.1 = (f32[2048,1152]{1,0:T(8,128)}, f32[2048,1152]{1,0:T(8,128)}, u32[]{:S(2)}, u32[]{:S(2)}) collective-permute-start(f32[2048,1152]{1,0:T(8,128)} %copy.16), channel_id=1, source_target_pairs={{0,1},{1,0},{2,3},{3,2},{4,5},{5,4},{6,7},{7,6},{8,9},{9,8},{10,11... | collective-permute-start | bytes 28311560 | tf_op jit(solution)/shard_map/ppermute | solution.py:93
  265.8 268.7 %copy-start.1 = (bf16[32,2,1152]{2,1,0:T(2,128)(2,1)S(1)}, bf16[32,2,1152]{2,1,0:T(2,128)(2,1)}, u32[]{:S(2)}) copy-start(bf16[32,2,1152]{2,1,0:T(2,128)(2,1)} %param.11) | copy-start | bytes 442372
  523.5 4.2 collective-permute-start.2
  528.7 4.9 collective-permute-start.3
Sparse Core Ops, SparseCore 0:
  11.8 95.1 all-gather.2
  265.9 257.5 reduce-scatter.1

commit v2 on v1

--- a/solution.py
+++ b/solution.py
@@ -1,6 +1,8 @@
 import jax
 import jax.numpy as jnp
+import numpy as np
 from jax import lax
+from jax.sharding import Mesh
 from jax.sharding import PartitionSpec as P
 
 BLOCK = 128
@@ -61,6 +63,10 @@
     return lax.fori_loop(jnp.int32(0), nblocks, block_step, (outputs, input_grads, start_grad))
 
 
+SHARD = ("y", "zh", "x")
+REP = ("zl", "c")
+
+
 def core_pairs(n):
     return [(i, i ^ 1) for i in range(n)]
 
@@ -70,8 +76,8 @@
 
 
 def local(rows_in, cotangent, expert_counts, weights):
-    nrep = lax.axis_size("rep")
-    core = lax.axis_index("rep") % 2
+    nrep = lax.axis_size(REP)
+    core = lax.axis_index("c")
     other = 1 - core
     counts = expert_counts[0]
     alive, padded, starts = alive_rows(counts, rows_in.shape[0])
@@ -81,8 +87,8 @@
     input_grads = jnp.zeros_like(rows_in)
 
     mine_local = lax.dynamic_index_in_dim(weights, core, 1, keepdims=False)
-    mine = lax.all_gather(mine_local, "shard", axis=0, tiled=True)
-    theirs = lax.ppermute(mine, "rep", core_pairs(nrep))
+    mine = lax.all_gather(mine_local, SHARD, axis=0, tiled=True)
+    theirs = lax.ppermute(mine, REP, core_pairs(nrep))
 
     outputs, input_grads, grad_mine = run_expert(
         mine, inputs, upstream, starts[core], padded[core] // BLOCK, outputs, input_grads
@@ -90,22 +96,35 @@
     outputs, input_grads, grad_theirs = run_expert(
         theirs, inputs, upstream, starts[other], padded[other] // BLOCK, outputs, input_grads
     )
-    grad_mine = grad_mine + lax.ppermute(grad_theirs, "rep", core_pairs(nrep))
-    part = lax.psum_scatter(grad_mine, "shard", scatter_dimension=0, tiled=True)
-    part = part + lax.ppermute(part, "rep", chip_pairs(nrep))
-    part_other = lax.ppermute(part, "rep", core_pairs(nrep))
+    grad_mine = grad_mine + lax.ppermute(grad_theirs, REP, core_pairs(nrep))
+    ny, nzh, nx = (lax.axis_size(a) for a in SHARD)
+    rows = grad_mine.shape[0] // (ny * nzh * nx)
+    part = grad_mine.reshape(ny, nzh, nx, rows, -1).transpose(2, 0, 1, 3, 4)
+    part = part.reshape(grad_mine.shape)
+    for axis in ("x", "y", "zh"):
+        part = lax.psum_scatter(part, axis, scatter_dimension=0, tiled=True)
+    part = part + lax.ppermute(part, REP, chip_pairs(nrep))
+    part_other = lax.ppermute(part, REP, core_pairs(nrep))
     first = jnp.where(core == 0, part, part_other)
     second = jnp.where(core == 0, part_other, part)
     reduced = jnp.stack([first, second], axis=1)
     return (outputs, input_grads, reduced)
 
 
+def physical_mesh(mesh):
+    devices = np.asarray(mesh.devices)
+    flat = devices.reshape(-1)
+    nx = len({d.coords[0] for d in flat})
+    ny = len({d.coords[1] for d in flat})
+    nshard, nrep = mesh.shape["shard"], mesh.shape["rep"]
+    shape = (ny, nshard // (nx * ny), nx, nrep // 2, 2)
+    return Mesh(devices.reshape(shape), SHARD + REP)
+
+
 def solution(mesh):
-    in_specs = (
-        P(("shard", "rep"), None),
-        P(("shard", "rep"), None),
-        P(("shard", "rep"), None),
-        P("shard", None, None),
+    rows = P(SHARD + REP, None)
+    in_specs = (rows, rows, rows, P(SHARD, None, None))
+    out_specs = (rows, rows, P(SHARD, None, None))
+    return jax.shard_map(
+        local, mesh=physical_mesh(mesh), in_specs=in_specs, out_specs=out_specs, check_vma=False
     )
-    out_specs = (P(("shard", "rep"), None), P(("shard", "rep"), None), P("shard", None, None))
-    return jax.shard_map(local, mesh=mesh, in_specs=in_specs, out_specs=out_specs, check_vma=False)

time: 543 us -> 447 us (0.82)
  waiting for transfers between devices: 354 us -> 283 us
  matrix products: 49 us -> 29.5 us
  other arithmetic: 46.3 us -> 39.4 us
    reduce_scatter x1 -> x3, waiting for transfers between devices: 258 us -> 187 us  [local(): part = lax.psum_scatter(part, axis, scatter_dimension=0, tiled=True)]
    transpose x0 -> x1, local copies, waits for them, and re-layouts: none -> 8.17 us  [local(): part = grad_mine.reshape(ny, nzh, nx, rows, -1).transpose(2, 0, 1, 3, 4)]
    add x4 -> x3, other arithmetic: 28.1 us -> 21.2 us  [block_step(): return (outputs, input_grads, grad_total + grad_piece)]
    dot_general x4 -> x3, matrix products: 12.1 us -> 5.32 us  [expert_block(): lax.dot_general(joint_grad, gate_up, (((1,), (1,)), ((), ())), preferred_...]
    dynamic_update_slice x4 -> x3, local copies, waits for them, and re-layouts: 14.8 us -> 11.4 us  [block_step(): lax.dynamic_update_slice_in_dim(input_grads, input_grad, row_begin, 0)]
    dynamic_update_slice x4 -> x3, local copies, waits for them, and re-layouts: 14.7 us -> 11.4 us  [block_step(): outputs = lax.dynamic_update_slice_in_dim(outputs, output, row_begin, 0)]
  transfers between devices with their start and end apart: 6 -> 8, of which waited for: 5 -> 7; matrix products, arithmetic and copies ran while one was open for 5% -> 16% of each run, Pallas kernels for 0% -> 0%
where the time goes in v2:
time: 447 us; the launch traced here: 445 us
  waiting for transfers between devices  283 us (63%)
  local copies, waits for them, and re-layouts  67.7 us (15%)
  other arithmetic  39.4 us (9%)
  matrix products  29.5 us (7%)
  between operations  19 us (4%)
  starting transfers between devices  4.75 us (1%)
    reduce_scatter x3, waiting for transfers between devices, local(): part = lax.psum_scatter(part, axis, scatter_dimension=0, tiled=True)  187 us
    all_gather x1, waiting for transfers between devices, local(): mine = lax.all_gather(mine_local, SHARD, axis=0, tiled=True)  85.9 us
    add x3, other arithmetic, block_step(): return (outputs, input_grads, grad_total + grad_piece)  21.2 us
    while x2, local copies, waits for them, and re-layouts, run_expert(): lax.fori_loop(jnp.int32(0), nblocks, block_step, (outputs, input_grads, s...  19.2 us
    another operation x4, local copies, waits for them, and re-layouts  12.9 us
    dynamic_update_slice x3, local copies, waits for them, and re-layouts, block_step(): lax.dynamic_update_slice_in_dim(input_grads, input_grad, row_begin, 0)  11.4 us
    dynamic_update_slice x3, local copies, waits for them, and re-layouts, block_step(): outputs = lax.dynamic_update_slice_in_dim(outputs, output, row_begin, 0)  11.4 us
    add x1, other arithmetic, local(): grad_mine = grad_mine + lax.ppermute(grad_theirs, REP, core_pairs(nrep))  11 us
  transfers between devices with their start and end apart: 8, of which 7 were waited for; matrix products, arithmetic and copies ran while one was open for 16% of the time, Pallas kernels for 0%

profile of v2, /device:TPU:1, one launch (start us, length us, event | category | flops | bytes accessed | tf_op | source)
XLA Modules:
  0.0 445.4 jit_solution(6185561289105867633)
XLA Ops:
  7.2 0.9 copy-done
  17.1 4.0 broadcast_select_fusion
  21.1 85.9 %all-gather.3.cloned.1.call-done = bf16[2048,1,1152]{2,0,1:T(8,128)(2,1)} async-done(((bf16[32,1,1152]{2,0,1:T(8,128)(2,1)}), bf16[2048,1,1152]{2,0,1:T(8,128)(2,1)}) %all-gather.3.cloned.1.call-update) | async-done | bytes 4718608 | tf_op jit(solution)/shard_map/all_gather | solution.py:90
  107.7 1.6 broadcast.130.clone
  109.3 1.6 broadcast.130
  110.9 4.9 %broadcast.131.clone = f32[2048,1152]{0,1:T(8,128)} broadcast(f32[]{:T(128)} %constant.72.clone.1), dimensions={} | broadcast | bytes 9437188 | tf_op jit(solution)/shard_map/broadcast.12
  115.7 49.1 %while.28 = (s32[]{:T(128)}, bf16[512,2048]{1,0:T(8,128)(2,1)}, bf16[512,2048]{1,0:T(8,128)(2,1)}, f32[2048,1152]{0,1:T(8,128)}, s32[]{:T(128)}, /*index=5*/s32[...) while((s32[]{:T(128)}, bf16[512,2048]{1,0:T(8,128)(2,1)}, ...), condition=%wide.region_3.4_spmd, body=%wide.region_2.3_spmd.sunk | while | flops 1818705920 | bytes 72974568 | solution.py:63
  116.3 2.6 fusion.87
  119.6 1.5 multiply_convert_fusion.8
  121.7 1.1 fusion.88
  122.9 3.8 dynamic_update_slice.17
  126.7 3.8 dynamic_update_slice.16
  130.5 1.7 fusion.89
  132.2 1.0 fusion.90
  133.2 7.1 %maximum_add_fusion.4 = f32[2048,1152]{0,1:T(8,128)} fusion(f32[2048,1152]{0,1:T(8,128)} %get-tuple-element.314, f32[2048,384]{0,1:T(8,128)S(1)} %fusion.89, f32[2048,768]{0,1:T(8,128)S(1)} %fusion.90), kind=kLoop, calls=%fused_computation.clone.1 | loop fusion | flops 4718592 | bytes 28311552 | tf_op jit(solution)/shard_map/while/body/add | solution.py:60
  140.9 2.6 fusion.87
  144.2 1.5 multiply_convert_fusion.8
  146.3 1.2 fusion.88
  147.5 3.8 dynamic_update_slice.17
  151.3 3.8 dynamic_update_slice.16
  155.1 1.7 fusion.89
  156.7 1.0 fusion.90
  157.8 7.1 %maximum_add_fusion.4 = f32[2048,1152]{0,1:T(8,128)} fusion(f32[2048,1152]{0,1:T(8,128)} %get-tuple-element.314, f32[2048,384]{0,1:T(8,128)S(1)} %fusion.89, f32[2048,768]{0,1:T(8,128)S(1)} %fusion.90), kind=kLoop, calls=%fused_computation.clone.1 | loop fusion | flops 4718592 | bytes 28311552 | tf_op jit(solution)/shard_map/while/body/add | solution.py:60
  164.9 4.8 %broadcast.131 = f32[2048,1152]{0,1:T(8,128)} broadcast(f32[]{:T(128)} %constant.72.clone.1), dimensions={} | broadcast | bytes 9437188 | tf_op jit(solution)/shard_map/broadcast.12
  169.7 27.6 %while.29 = (s32[]{:T(128)}, bf16[512,2048]{1,0:T(8,128)(2,1)}, bf16[512,2048]{1,0:T(8,128)(2,1)}, f32[2048,1152]{0,1:T(8,128)}, s32[]{:T(128)}, /*index=5*/s32[...) while((s32[]{:T(128)}, bf16[512,2048]{1,0:T(8,128)(2,1)}, ...), condition=%wide.region_5.6_spmd, body=%wide.region_4.5_spmd.sunk | while | flops 1818705920 | bytes 54100176 | solution.py:63
  170.4 2.5 fusion.99
  172.9 2.0 multiply_convert_fusion.9
  174.9 2.0 convolution_convert_fusion.5
  177.0 3.0 fusion.100
  180.0 3.8 dynamic_update_slice.19
  183.8 3.8 dynamic_update_slice.18
  187.6 1.7 fusion.101
  189.3 1.0 fusion.102
  190.3 7.0 %maximum_add_fusion.5 = f32[2048,1152]{0,1:T(8,128)} fusion(f32[2048,1152]{0,1:T(8,128)} %get-tuple-element.353, f32[2048,384]{0,1:T(8,128)S(1)} %fusion.101, f32[2048,768]{0,1:T(8,128)S(1)} %fusion.102), kind=kLoop, calls=%fused_computation.28.clone.1 | loop fusion | flops 4718592 | bytes 28311552 | tf_op jit(solution)/shard_map/while/body/add | solution.py:60
  197.3 9.6 %copy.20 = f32[2048,1152]{1,0:T(8,128)} copy(f32[2048,1152]{0,1:T(8,128)} %get-tuple-element.108) | data formatting | bytes 18874368 | tf_op jit(solution)/shard_map/while | solution.py:63
  207.0 9.6 %copy.21 = f32[2048,1152]{1,0:T(8,128)} copy(f32[2048,1152]{0,1:T(8,128)} %get-tuple-element.107) | data formatting | bytes 18874368 | tf_op jit(solution)/shard_map/while | solution.py:63
  216.6 5.4 %collective-permute-done.1 = f32[2048,1152]{1,0:T(8,128)} collective-permute-done((f32[2048,1152]{1,0:T(8,128)}, f32[2048,1152]{1,0:T(8,128)}, u32[]{:S(2)}, u32[]{:S(2)}) %collective-permute-start.1) | collective-permute-done | bytes 9437216 | tf_op jit(solution)/shard_map/ppermute | solution.py:99
  222.0 11.0 %add.106 = f32[2048,1152]{1,0:T(8,128)} add(f32[2048,1152]{1,0:T(8,128)} %copy.21, f32[2048,1152]{1,0:T(8,128)} %collective-permute-done.1) | non-fusion elementwise | flops 2359296 | bytes 28311552 | tf_op jit(solution)/shard_map/add | solution.py:99
  232.9 8.2 %copy.22 = f32[4,4,4,32,1152]{4,3,2,1,0:T(8,128)} copy(f32[4,4,4,32,1152]{4,3,0,2,1:T(8,128)} %bitcast.54) | data formatting | bytes 18874368 | tf_op jit(solution)/shard_map/transpose | solution.py:102
  241.2 121.4 %reduce-scatter.4.cloned.1.call-done = f32[512,1152]{1,0:T(8,128)} async-done(((f32[2048,1152]{1,0:T(8,128)}), f32[512,1152]{1,0:T(8,128)}) %reduce-scatter.4.cloned.1.call-update) | async-done | bytes 2359312 | tf_op jit(solution)/shard_map/reduce_scatter | solution.py:105
  362.7 36.7 %reduce-scatter.6.cloned.1.call-done = f32[128,1152]{1,0:T(8,128)} async-done(((f32[512,1152]{1,0:T(8,128)}), f32[128,1152]{1,0:T(8,128)}) %reduce-scatter.6.cloned.1.call-update) | async-done | bytes 589840 | tf_op jit(solution)/shard_map/reduce_scatter | solution.py:105
  399.4 29.2 %reduce-scatter.8.cloned.1.call-done = f32[32,1152]{1,0:T(8,128)} async-done(((f32[128,1152]{1,0:T(8,128)}), f32[32,1152]{1,0:T(8,128)}) %reduce-scatter.8.cloned.1.call-update) | async-done | bytes 147472 | tf_op jit(solution)/shard_map/reduce_scatter | solution.py:105
  428.6 0.8 collective-permute-start.2
  429.3 3.4 collective-permute-done.2
  432.8 0.9 add.107
  433.7 3.1 collective-permute-start.3
  436.8 1.0 collective-permute-done.3
  437.9 0.9 copy.23
  (30 shorter events, 7.3 us)
Async XLA Ops:
  7.2 0.9 copy-start
  7.2 99.8 %all-gather.3.cloned.1.call-start = ((), (), s32[]{:S(2)}) async-start(), calls=%async_computation.6 | async-start | bytes 4792320 | tf_op jit(solution)/shard_map/all_gather | solution.py:90
  8.9 353.7 %reduce-scatter.4.cloned.1.call-start = ((), (), s32[]{:S(2)}) async-start(), calls=%async_computation.3 | async-start | bytes 11796480 | tf_op jit(solution)/shard_map/reduce_scatter | solution.py:105
  107.0 57.9 %collective-permute-start = (bf16[2048,1152]{1,0:T(8,128)(2,1)}, bf16[2048,1152]{1,0:T(8,128)(2,1)}, u32[]{:S(2)}, u32[]{:S(2)}) collective-permute-start(bf16[2048,1152]{1,0:T(8,128)(2,1)} %bitcast.56), channel_id=1, source_target_pairs={{0,1},{1,0},{2,3},{3,2},{4,5},{5,4},{6,7},{7,6},{8,9},{9,8},{10,11... | collective-permute-start | bytes 14155784 | tf_op jit(solution)/shard_map/ppermute | solution.py:91
  116.3 3.3 copy-start.2
  140.9 3.3 copy-start.2
  207.0 15.0 %collective-permute-start.1 = (f32[2048,1152]{1,0:T(8,128)}, f32[2048,1152]{1,0:T(8,128)}, u32[]{:S(2)}, u32[]{:S(2)}) collective-permute-start(f32[2048,1152]{1,0:T(8,128)} %copy.20), channel_id=1, source_target_pairs={{0,1},{1,0},{2,3},{3,2},{4,5},{5,4},{6,7},{7,6},{8,9},{9,8},{10,11... | collective-permute-start | bytes 28311560 | tf_op jit(solution)/shard_map/ppermute | solution.py:99
  241.1 197.7 %copy-start.1 = (bf16[32,2,1152]{2,1,0:T(2,128)(2,1)S(1)}, bf16[32,2,1152]{2,1,0:T(2,128)(2,1)}, u32[]{:S(2)}) copy-start(bf16[32,2,1152]{2,1,0:T(2,128)(2,1)} %param.11) | copy-start | bytes 442372
  241.1 158.2 %reduce-scatter.6.cloned.1.call-start = ((), (), s32[]{:S(2)}) async-start(), calls=%async_computation.4 | async-start | bytes 2949120 | tf_op jit(solution)/shard_map/reduce_scatter | solution.py:105
  362.6 65.9 %reduce-scatter.8.cloned.1.call-start = ((), (), s32[]{:S(2)}) async-start(), calls=%async_computation.5 | async-start | bytes 737280 | tf_op jit(solution)/shard_map/reduce_scatter | solution.py:105
  428.6 4.2 collective-permute-start.2
  433.7 4.1 collective-permute-start.3
Sparse Core Ops, SparseCore 0:
  11.8 95.1 all-gather.2
  241.3 121.3 reduce-scatter.3
  365.2 34.1 reduce-scatter.5
  401.8 26.7 reduce-scatter.7

commit v3 on v2

--- a/solution.py
+++ b/solution.py
@@ -37,30 +37,10 @@
     return (output, input_grad, jnp.concatenate([proj_grad, down_grad], axis=1))
 
 
-def alive_rows(counts, total_rows):
-    padded = (counts + BLOCK - 1) // BLOCK * BLOCK
-    starts = jnp.cumsum(padded) - padded
-    position = jnp.arange(total_rows, dtype=jnp.int32)
-    inside = (position[:, None] >= starts[None, :]) & (
-        position[:, None] < (starts + counts)[None, :]
-    )
-    return (jnp.any(inside, axis=1), padded, starts)
-
-
-def run_expert(expert_slab, inputs, upstream, start_row, nblocks, outputs, input_grads):
-
-    def block_step(block_index, state):
-        outputs, input_grads, grad_total = state
-        row_begin = start_row + block_index * BLOCK
-        block_in = lax.dynamic_slice_in_dim(inputs, row_begin, BLOCK, 0)
-        block_up = lax.dynamic_slice_in_dim(upstream, row_begin, BLOCK, 0)
-        output, input_grad, grad_piece = expert_block(block_in, block_up, expert_slab)
-        outputs = lax.dynamic_update_slice_in_dim(outputs, output, row_begin, 0)
-        input_grads = lax.dynamic_update_slice_in_dim(input_grads, input_grad, row_begin, 0)
-        return (outputs, input_grads, grad_total + grad_piece)
-
-    start_grad = jnp.zeros(expert_slab.shape, jnp.float32)
-    return lax.fori_loop(jnp.int32(0), nblocks, block_step, (outputs, input_grads, start_grad))
+def run_expert(expert_slab, inputs, upstream, rows):
+    inputs = jnp.where(rows[:, None], inputs, jnp.zeros_like(inputs))
+    upstream = jnp.where(rows[:, None], upstream, jnp.zeros_like(upstream))
+    return expert_block(inputs, upstream, expert_slab)
 
 
 SHARD = ("y", "zh", "x")
@@ -80,26 +60,30 @@
     core = lax.axis_index("c")
     other = 1 - core
     counts = expert_counts[0]
-    alive, padded, starts = alive_rows(counts, rows_in.shape[0])
-    inputs = jnp.where(alive[:, None], rows_in, jnp.zeros_like(rows_in))
-    upstream = jnp.where(alive[:, None], cotangent, jnp.zeros_like(cotangent))
-    outputs = jnp.zeros_like(rows_in)
-    input_grads = jnp.zeros_like(rows_in)
+    padded = (counts + BLOCK - 1) // BLOCK * BLOCK
+    starts = jnp.cumsum(padded) - padded
+    position = jnp.arange(rows_in.shape[0], dtype=jnp.int32)
+    live = (position[:, None] >= starts[None, :]) & (position[:, None] < (starts + counts)[None, :])
+    live_mine = jnp.where(core == 0, live[:, 0], live[:, 1])
+    live_theirs = jnp.where(core == 0, live[:, 1], live[:, 0])
 
     mine_local = lax.dynamic_index_in_dim(weights, core, 1, keepdims=False)
     mine = lax.all_gather(mine_local, SHARD, axis=0, tiled=True)
     theirs = lax.ppermute(mine, REP, core_pairs(nrep))
 
-    outputs, input_grads, grad_mine = run_expert(
-        mine, inputs, upstream, starts[core], padded[core] // BLOCK, outputs, input_grads
+    out_mine, in_grad_mine, grad_mine = run_expert(mine, rows_in, cotangent, live_mine)
+    out_theirs, in_grad_theirs, grad_theirs = run_expert(theirs, rows_in, cotangent, live_theirs)
+    zero = jnp.zeros_like(rows_in)
+    outputs = jnp.where(
+        live_mine[:, None], out_mine, jnp.where(live_theirs[:, None], out_theirs, zero)
     )
-    outputs, input_grads, grad_theirs = run_expert(
-        theirs, inputs, upstream, starts[other], padded[other] // BLOCK, outputs, input_grads
+    input_grads = jnp.where(
+        live_mine[:, None], in_grad_mine, jnp.where(live_theirs[:, None], in_grad_theirs, zero)
     )
-    grad_mine = grad_mine + lax.ppermute(grad_theirs, REP, core_pairs(nrep))
     ny, nzh, nx = (lax.axis_size(a) for a in SHARD)
     rows = grad_mine.shape[0] // (ny * nzh * nx)
-    part = grad_mine.reshape(ny, nzh, nx, rows, -1).transpose(2, 0, 1, 3, 4)
+    part = grad_mine + lax.ppermute(grad_theirs, REP, core_pairs(nrep))
+    part = part.reshape(ny, nzh, nx, rows, -1).transpose(2, 0, 1, 3, 4)
     part = part.reshape(grad_mine.shape)
     for axis in ("x", "y", "zh"):
         part = lax.psum_scatter(part, axis, scatter_dimension=0, tiled=True)

time: 447 us -> 348 us (0.78)
  local copies, waits for them, and re-layouts: 67.7 us -> 21.1 us
  waiting for transfers between devices: 283 us -> 254 us
  other arithmetic: 39.4 us -> 13 us
  matrix products: 29.5 us -> 41.6 us
  between operations: 19 us -> 13.9 us
    reduce_scatter x3, waiting for transfers between devices: 187 us -> 146 us  [local(): part = lax.psum_scatter(part, axis, scatter_dimension=0, tiled=True)]
    add x4 -> x1, other arithmetic: 32.2 us -> 4.69 us  [local(): part = grad_mine + lax.ppermute(grad_theirs, REP, core_pairs(nrep))]
    dynamic_update_slice x6 -> x0, local copies, waits for them, and re-layouts: 22.8 us -> none  [the longest x3 11.4 us: block_step(): lax.dynamic_update_slice_in_dim(input_grads, input_grad, row_begin, 0)]
    while x6 -> x0, local copies, waits for them, and re-layouts: 20.5 us -> none  [the longest x2 19.2 us: run_expert(): lax.fori_loop(jnp.int32(0), nblocks, block_step, (outputs, input_grads, s...]
    another operation x4 -> x0, local copies, waits for them, and re-layouts: 12.9 us -> none
    all_gather x1, waiting for transfers between devices: 85.9 us -> 98 us  [local(): mine = lax.all_gather(mine_local, SHARD, axis=0, tiled=True)]
    add x0 -> x1, local copies, waits for them, and re-layouts: none -> 9.77 us  [local(): part = grad_mine + lax.ppermute(grad_theirs, REP, core_pairs(nrep))]
    concatenate x0 -> x1, other arithmetic: none -> 6.62 us  [expert_block(): return (output, input_grad, jnp.concatenate([proj_grad, down_grad], axis=1))]
  transfers between devices with their start and end apart: 8 -> 8, of which waited for: 7 -> 6; matrix products, arithmetic and copies ran while one was open for 16% -> 9% of each run, Pallas kernels for 0% -> 0%
where the time goes in v3:
time: 348 us; the launch traced here: 347 us
  waiting for transfers between devices  254 us (73%)
  matrix products  41.6 us (12%)
  local copies, waits for them, and re-layouts  21.1 us (6%)
  between operations  13.9 us (4%)
  other arithmetic  13 us (4%)
  starting transfers between devices  3.52 us (1%)
    reduce_scatter x3, waiting for transfers between devices, local(): part = lax.psum_scatter(part, axis, scatter_dimension=0, tiled=True)  146 us
    all_gather x1, waiting for transfers between devices, local(): mine = lax.all_gather(mine_local, SHARD, axis=0, tiled=True)  98 us
    dot_general x2, matrix products, expert_block(): lax.dot_general(joint_grad, gate_up, (((1,), (1,)), ((), ())), preferred_...  10.8 us
    add x1, local copies, waits for them, and re-layouts, local(): part = grad_mine + lax.ppermute(grad_theirs, REP, core_pairs(nrep))  9.77 us
    dot_general x2, matrix products, expert_block(): project = jnp.dot(inputs, gate_up, preferred_element_type=jnp.float32)  9.01 us
    transpose x1, local copies, waits for them, and re-layouts, local(): part = part.reshape(ny, nzh, nx, rows, -1).transpose(2, 0, 1, 3, 4)  8.18 us
    dot_general x2, matrix products, expert_block(): lax.dot_general(hidden, down_t, (((1,), (1,)), ((), ())), preferred_eleme...  8.09 us
  transfers between devices with their start and end apart: 8, of which 6 were waited for; matrix products, arithmetic and copies ran while one was open for 9% of the time, Pallas kernels for 0%

profile of v3, /device:TPU:1, one launch (start us, length us, event | category | flops | bytes accessed | tf_op | source)
XLA Modules:
  0.0 347.1 jit_solution(13988858479651455887)
XLA Ops:
  7.2 0.0 copy-start
  7.2 0.0 all-gather.3.cloned.1.call-start
  7.2 0.9 copy-done
  8.1 0.2 constant_dynamic-slice_fusion
  8.2 0.6 copy.30
  8.9 0.0 all-gather.3.cloned.1.call-update
  8.9 0.0 reduce-scatter.4.cloned.1.call-start
  9.0 98.0 %all-gather.3.cloned.1.call-done = bf16[2048,1,1152]{2,0,1:T(8,128)(2,1)} async-done(((bf16[32,1,1152]{2,0,1:T(8,128)(2,1)}), bf16[2048,1,1152]{2,0,1:T(8,128)(2,1)}) %all-gather.3.cloned.1.call-update) | async-done | bytes 4718608 | tf_op jit(solution)/shard_map/all_gather | solution.py:71
  107.0 0.7 collective-permute-start
  107.7 0.7 fusion.26
  108.4 0.2 reduce-window_clone.1
  108.6 0.7 subtract_bitcast_fusion
  109.2 0.1 compare_and_fusion
  109.3 6.3 %collective-permute-done = bf16[2048,1152]{1,0:T(8,128)(2,1)} collective-permute-done((bf16[2048,1152]{1,0:T(8,128)(2,1)}, bf16[2048,1152]{1,0:T(8,128)(2,1)}, u32[]{:S(2)}, u32[]{:S(2)}) %collective-permute-start) | collective-permute-done | bytes 4718624 | tf_op jit(solution)/shard_map/ppermute | solution.py:72
  115.6 4.5 %fusion.1 = f32[512,768]{1,0:T(8,128)S(1)} fusion(bf16[2048,1152]{1,0:T(8,128)(2,1)} %collective-permute-done, bf16[512,2048]{1,0:T(8,128)(2,1)} %param.4, pred[512]{0:T(512)(128)(4,1)S(1)} %get-tuple-element.9), kind=kOutput, calls=%fused_computation.7 | convolution fusion | flops 1611661312 | bytes 6816256 | tf_op jit(solution)/shard_map/dot_general | solution.py:15
  120.1 3.0 multiply_convert_fusion.1
  123.1 0.0 copy-start.2
  123.1 2.7 fusion.23
  125.9 1.9 fusion.22
  127.8 6.6 %pad_maximum_fusion = f32[2048,1152]{0,1:T(8,128)} fusion(f32[2048,384]{0,1:T(8,128)} %fusion.23, f32[2048,768]{0,1:T(8,128)S(1)} %fusion.22), kind=kLoop, calls=%fused_computation.1 | loop fusion | flops 2359296 | bytes 18874368 | tf_op jit(solution)/shard_map/concatenate | solution.py:37
  134.5 0.4 collective-permute-start.1
  134.8 4.5 %fusion.4 = f32[512,768]{1,0:T(8,128)S(1)} fusion(bf16[2048,1152]{1,0:T(8,128)(2,1)} %bitcast.20, bf16[512,2048]{1,0:T(8,128)(2,1)} %param.4, pred[512]{0:T(512)(128)(4,1)S(1)} %get-tuple-element.10), kind=kOutput, calls=%fused_computation.10 | convolution fusion | flops 1611661312 | bytes 6816256 | tf_op jit(solution)/shard_map/dot_general | solution.py:15
  139.4 3.0 multiply_convert_fusion.3
  142.3 0.0 copy-start.3
  142.4 1.1 fusion.21
  143.4 0.5 copy-done.3
  143.9 2.0 fusion.20
  145.9 3.4 collective-permute-done.1
  149.3 4.7 %maximum_add_fusion = f32[2048,1152]{0,1:T(8,128)} fusion(f32[2048,1152]{0,1:T(8,128)S(1)} %collective-permute-done.1, f32[2048,384]{0,1:T(8,128)S(1)} %fusion.21, f32[2048,768]{0,1:T(8,128)S(1)} %fusion.20), kind=kLoop, calls=%fused_computation | loop fusion | flops 4718592 | bytes 28311552 | tf_op jit(solution)/shard_map/add | solution.py:85
  154.0 9.8 %copy.25 = f32[2048,1152]{1,0:T(8,128)} copy(f32[2048,1152]{0,1:T(8,128)} %maximum_add_fusion) | data formatting | bytes 18874368 | tf_op jit(solution)/shard_map/add | solution.py:85
  163.8 8.2 %copy.26 = f32[4,4,4,32,1152]{4,3,2,1,0:T(8,128)} copy(f32[4,4,4,32,1152]{4,3,0,2,1:T(8,128)} %bitcast.18) | data formatting | bytes 18874368 | tf_op jit(solution)/shard_map/transpose | solution.py:86
  172.0 0.0 reduce-scatter.4.cloned.1.call-update
  172.0 0.0 reduce-scatter.6.cloned.1.call-start
  172.0 89.5 %reduce-scatter.4.cloned.1.call-done = f32[512,1152]{1,0:T(8,128)} async-done(((f32[2048,1152]{1,0:T(8,128)}), f32[512,1152]{1,0:T(8,128)}) %reduce-scatter.4.cloned.1.call-update) | async-done | bytes 2359312 | tf_op jit(solution)/shard_map/reduce_scatter | solution.py:89
  261.5 0.0 reduce-scatter.6.cloned.1.call-update
  261.5 0.0 reduce-scatter.8.cloned.1.call-start
  261.6 36.7 %reduce-scatter.6.cloned.1.call-done = f32[128,1152]{1,0:T(8,128)} async-done(((f32[512,1152]{1,0:T(8,128)}), f32[128,1152]{1,0:T(8,128)}) %reduce-scatter.6.cloned.1.call-update) | async-done | bytes 589840 | tf_op jit(solution)/shard_map/reduce_scatter | solution.py:89
  298.3 0.0 reduce-scatter.8.cloned.1.call-update
  298.3 4.0 %convolution_convert_fusion.3 = bf16[512,2048]{1,0:T(8,128)(2,1)} fusion(bf16[512,384]{1,0:T(8,128)(2,1)S(1)} %get-tuple-element.16, bf16[2048,1152]{1,0:T(8,128)(2,1)} %bitcast.22), kind=kOutput, calls=%fused_computation.5 | convolution fusion | flops 806354944 | bytes 4063232 | tf_op jit(solution)/shard_map/dot_general | solution.py:21
  302.3 5.1 %convolution_convert_fusion.1 = bf16[512,2048]{1,0:T(8,128)(2,1)} fusion(bf16[2048,1152]{1,0:T(8,128)(2,1)} %bitcast.23, bf16[512,384]{1,0:T(8,128)(2,1)S(1)} %get-tuple-element.14, bf16[512,384]{1,0:T(8,128)(2,1)S(1)} %get-tuple-element.13), kind=kOutput, calls=%fused_computation.3 | convolution fusion | flops 1613234176 | bytes 6029312 | tf_op jit(solution)/shard_map/dot_general | solution.py:34
  307.4 20.0 %reduce-scatter.8.cloned.1.call-done = f32[32,1152]{1,0:T(8,128)} async-done(((f32[128,1152]{1,0:T(8,128)}), f32[32,1152]{1,0:T(8,128)}) %reduce-scatter.8.cloned.1.call-update) | async-done | bytes 147472 | tf_op jit(solution)/shard_map/reduce_scatter | solution.py:89
  327.5 0.8 collective-permute-start.2
  328.3 5.7 %fusion.10 = bf16[512,2048]{1,0:T(8,128)(2,1)} fusion(bf16[512,2048]{1,0:T(8,128)(2,1)} %convolution_convert_fusion.1, bf16[2048,1152]{1,0:T(8,128)(2,1)} %collective-permute-done, pred[512]{0:T(512)(128)(4,1)S(1)} %get-tuple-element.9, pred[512]{0:T(512)(128)(4,1)S(1)} %get-tuple-element.10, bf16[512,384]{1,0:T(8,128)(2,1)S(1)} %copy-done.7, ...), kind=kOutput, calls=%fused_computation.14 | convolution fusion | flops 1615331328 | bytes 8127488 | tf_op jit(solution)/shard_map/dot_general | solution.py:34
  334.0 0.0 collective-permute-done.2
  334.0 1.5 collective-permute-start.3
  335.5 4.1 %fusion.13 = bf16[512,2048]{1,0:T(8,128)(2,1)} fusion(bf16[512,2048]{1,0:T(8,128)(2,1)S(1)} %copy-done.11, bf16[512,384]{1,0:T(8,128)(2,1)S(1)} %copy-done.13, pred[512]{0:T(512)(128)(4,1)S(1)} %get-tuple-element.9, pred[512]{0:T(512)(128)(4,1)S(1)} %get-tuple-element.10, bf16[2048,1152]{1,0:T(8,128)(2,1)} %collective-permute-done), kind=kOutput, calls=%fused_computation.15 | convolution fusion | flops 808452096 | bytes 6161408 | tf_op jit(solution)/shard_map/dot_general | solution.py:21
  339.6 0.0 collective-permute-done.3
  339.6 0.9 copy.27
  (27 shorter events, 0.1 us)
Async XLA Ops:
  7.2 0.9 copy-start
  7.2 99.8 %all-gather.3.cloned.1.call-start = ((), (), s32[]{:S(2)}) async-start(), calls=%async_computation.6 | async-start | bytes 4792320 | tf_op jit(solution)/shard_map/all_gather | solution.py:71
  8.9 252.6 %reduce-scatter.4.cloned.1.call-start = ((), (), s32[]{:S(2)}) async-start(), calls=%async_computation.3 | async-start | bytes 11796480 | tf_op jit(solution)/shard_map/reduce_scatter | solution.py:89
  107.0 8.6 %collective-permute-start = (bf16[2048,1152]{1,0:T(8,128)(2,1)}, bf16[2048,1152]{1,0:T(8,128)(2,1)}, u32[]{:S(2)}, u32[]{:S(2)}) collective-permute-start(bf16[2048,1152]{1,0:T(8,128)(2,1)} %bitcast.19), channel_id=1, source_target_pairs={{0,1},{1,0},{2,3},{3,2},{4,5},{5,4},{6,7},{7,6},{8,9},{9,8},{10,11... | collective-permute-start | bytes 14155784 | tf_op jit(solution)/shard_map/ppermute | solution.py:72
  115.6 4.5 %copy-start.9 = (bf16[512,2048]{1,0:T(8,128)(2,1)S(1)}, bf16[512,2048]{1,0:T(8,128)(2,1)}, u32[]{:S(2)}) copy-start(bf16[512,2048]{1,0:T(8,128)(2,1)} %param.5) | copy-start | bytes 6291460
  123.1 2.8 copy-start.12
  123.1 2.8 copy-start.4
  123.1 2.8 copy-start.6
  123.1 2.8 copy-start.2
  134.5 14.9 %collective-permute-start.1 = (f32[2048,1152]{0,1:T(8,128)}, f32[2048,1152]{0,1:T(8,128)S(1)}, u32[]{:S(2)}, u32[]{:S(2)}) collective-permute-start(f32[2048,1152]{0,1:T(8,128)} %pad_maximum_fusion), channel_id=1, source_target_pairs={{0,1},{1,0},{2,3},{3,2},{4,5},{5,4},{6,7},{7,6},{8,9},{9,8},{10,11... | collective-permute-start | bytes 28311560 | tf_op jit(solution)/shard_map/ppermute | solution.py:85
  134.8 4.5 %copy-start.10 = (bf16[512,2048]{1,0:T(8,128)(2,1)S(1)}, bf16[512,2048]{1,0:T(8,128)(2,1)}, u32[]{:S(2)}) copy-start(bf16[512,2048]{1,0:T(8,128)(2,1)} %param.5) | copy-start | bytes 6291460
  142.3 1.6 copy-start.3
  172.0 126.3 %reduce-scatter.6.cloned.1.call-start = ((), (), s32[]{:S(2)}) async-start(), calls=%async_computation.4 | async-start | bytes 2949120 | tf_op jit(solution)/shard_map/reduce_scatter | solution.py:89
  261.5 66.0 %reduce-scatter.8.cloned.1.call-start = ((), (), s32[]{:S(2)}) async-start(), calls=%async_computation.5 | async-start | bytes 737280 | tf_op jit(solution)/shard_map/reduce_scatter | solution.py:89
  302.3 25.9 %copy-start.5 = (bf16[512,384]{1,0:T(8,128)(2,1)S(1)}, bf16[512,384]{1,0:T(8,128)(2,1)}, u32[]{:S(2)}) copy-start(bf16[512,384]{1,0:T(8,128)(2,1)} %copy-done.4) | copy-start | bytes 1179652
  302.3 25.9 %copy-start.7 = (bf16[512,384]{1,0:T(8,128)(2,1)S(1)}, bf16[512,384]{1,0:T(8,128)(2,1)}, u32[]{:S(2)}) copy-start(bf16[512,384]{1,0:T(8,128)(2,1)} %copy-done.6) | copy-start | bytes 1179652
  307.4 28.1 %copy-start.11 = (bf16[512,2048]{1,0:T(8,128)(2,1)S(1)}, bf16[512,2048]{1,0:T(8,128)(2,1)}, u32[]{:S(2)}) copy-start(bf16[512,2048]{1,0:T(8,128)(2,1)} %convolution_convert_fusion.3) | copy-start | bytes 6291460
  327.5 6.5 %copy-start.8 = (f32[32,1152]{1,0:T(8,128)S(1)}, f32[32,1152]{1,0:T(8,128)}, u32[]{:S(2)}) copy-start(f32[32,1152]{1,0:T(8,128)} %reduce-scatter.8.cloned.1.call-done) | copy-start | bytes 442372
  327.5 8.0 %copy-start.13 = (bf16[512,384]{1,0:T(8,128)(2,1)S(1)}, bf16[512,384]{1,0:T(8,128)(2,1)}, u32[]{:S(2)}) copy-start(bf16[512,384]{1,0:T(8,128)(2,1)} %copy-done.12) | copy-start | bytes 1179652
  327.5 6.5 %collective-permute-start.2 = (f32[32,1152]{1,0:T(8,128)}, f32[32,1152]{1,0:T(8,128)S(1)}, u32[]{:S(2)}, u32[]{:S(2)}) collective-permute-start(f32[32,1152]{1,0:T(8,128)} %reduce-scatter.8.cloned.1.call-done), channel_id=1, source_target_pairs={{0,2},{1,3},{2,0},{3,1},{4,6},{5,7},{6,4},{7,5},{8,10},{9,11},{10,... | collective-permute-start | bytes 442376 | tf_op jit(solution)/shard_map/ppermute | solution.py:90
  334.0 5.6 %collective-permute-start.3 = (f32[32,1152]{1,0:T(8,128)S(1)}, f32[32,1152]{1,0:T(8,128)S(1)}, u32[]{:S(2)}, u32[]{:S(2)}) collective-permute-start(f32[32,1152]{1,0:T(8,128)S(1)} %add.65), channel_id=1, source_target_pairs={{0,1},{1,0},{2,3},{3,2},{4,5},{5,4},{6,7},{7,6},{8,9},{9,8},{10,11... | collective-permute-start | bytes 442376 | tf_op jit(solution)/shard_map/ppermute | solution.py:91
  335.5 5.1 %copy-start.1 = (bf16[32,2,1152]{2,1,0:T(2,128)(2,1)S(1)}, bf16[32,2,1152]{2,1,0:T(2,128)(2,1)}, u32[]{:S(2)}) copy-start(bf16[32,2,1152]{2,1,0:T(2,128)(2,1)} %param.7) | copy-start | bytes 442372
Sparse Core Ops, SparseCore 0:
  11.8 95.1 all-gather.2
  172.1 89.3 reduce-scatter.3
  264.1 34.1 reduce-scatter.5
  300.7 26.7 reduce-scatter.7

commit v4 on v3

--- a/solution.py
+++ b/solution.py
@@ -58,7 +58,6 @@
 def local(rows_in, cotangent, expert_counts, weights):
     nrep = lax.axis_size(REP)
     core = lax.axis_index("c")
-    other = 1 - core
     counts = expert_counts[0]
     padded = (counts + BLOCK - 1) // BLOCK * BLOCK
     starts = jnp.cumsum(padded) - padded
@@ -68,7 +67,9 @@
     live_theirs = jnp.where(core == 0, live[:, 1], live[:, 0])
 
     mine_local = lax.dynamic_index_in_dim(weights, core, 1, keepdims=False)
-    mine = lax.all_gather(mine_local, SHARD, axis=0, tiled=True)
+    mine = mine_local
+    for axis in ("x", "zh", "y"):
+        mine = gather_axis(mine, axis)
     theirs = lax.ppermute(mine, REP, core_pairs(nrep))
 
     out_mine, in_grad_mine, grad_mine = run_expert(mine, rows_in, cotangent, live_mine)
@@ -86,13 +87,40 @@
     part = part.reshape(ny, nzh, nx, rows, -1).transpose(2, 0, 1, 3, 4)
     part = part.reshape(grad_mine.shape)
     for axis in ("x", "y", "zh"):
-        part = lax.psum_scatter(part, axis, scatter_dimension=0, tiled=True)
+        part = scatter_axis(part, axis)
     part = part + lax.ppermute(part, REP, chip_pairs(nrep))
     part_other = lax.ppermute(part, REP, core_pairs(nrep))
     first = jnp.where(core == 0, part, part_other)
     second = jnp.where(core == 0, part_other, part)
     reduced = jnp.stack([first, second], axis=1)
     return (outputs, input_grads, reduced)
+
+
+def shift_pairs(n, k):
+    return [(j, (j + k) % n) for j in range(n)]
+
+
+def gather_axis(a, axis):
+    n = lax.axis_size(axis)
+    i = lax.axis_index(axis)
+    rows = a.shape[0]
+    out = jnp.zeros((n * rows,) + a.shape[1:], a.dtype)
+    out = lax.dynamic_update_slice_in_dim(out, a, i * rows, 0)
+    for k in range(1, n):
+        got = lax.ppermute(a, axis, shift_pairs(n, k))
+        out = lax.dynamic_update_slice_in_dim(out, got, ((i - k) % n) * rows, 0)
+    return out
+
+
+def scatter_axis(a, axis):
+    n = lax.axis_size(axis)
+    i = lax.axis_index(axis)
+    rows = a.shape[0] // n
+    total = lax.dynamic_slice_in_dim(a, i * rows, rows, 0)
+    for k in range(1, n):
+        chunk = lax.dynamic_slice_in_dim(a, ((i + k) % n) * rows, rows, 0)
+        total = total + lax.ppermute(chunk, axis, shift_pairs(n, k))
+    return total
 
 
 def physical_mesh(mesh):

time: 348 us -> 345 us (level)
  waiting for transfers between devices: 254 us -> 214 us
  starting transfers between devices: 3.52 us -> 39.2 us
  between operations: 13.9 us -> 0.96 us
  local copies, waits for them, and re-layouts: 21.1 us -> 33.2 us
  other arithmetic: 13 us -> 19.8 us
  matrix products: 41.6 us -> 37.8 us
    ppermute x0 -> x18, waiting for transfers between devices: none -> 202 us  [the longest x9 131 us: scatter_axis(): total = total + lax.ppermute(chunk, axis, shift_pairs(n, k))]
    reduce_scatter x3 -> x0, waiting for transfers between devices: 146 us -> none  [local(): part = lax.psum_scatter(part, axis, scatter_dimension=0, tiled=True)]
    all_gather x1 -> x0, waiting for transfers between devices: 98 us -> none  [local(): mine = lax.all_gather(mine_local, SHARD, axis=0, tiled=True)]
    ppermute x0 -> x18, starting transfers between devices: none -> 33.2 us  [the longest x9 21.7 us: gather_axis(): got = lax.ppermute(a, axis, shift_pairs(n, k))]
    dynamic_update_slice x0 -> x12, local copies, waits for them, and re-layouts: none -> 7.37 us  [the longest x9 6.14 us: gather_axis(): out = lax.dynamic_update_slice_in_dim(out, got, (i - k) % n * rows, 0)]
    add x0 -> x3, other arithmetic: none -> 5.73 us  [scatter_axis(): total = total + lax.ppermute(chunk, axis, shift_pairs(n, k))]
    dynamic_slice x0 -> x3, local copies, waits for them, and re-layouts: none -> 4.21 us  [scatter_axis(): chunk = lax.dynamic_slice_in_dim(a, (i + k) % n * rows, rows, 0)]
    transpose x1, local copies, waits for them, and re-layouts: 8.18 us -> 4.29 us  [local(): part = part.reshape(ny, nzh, nx, rows, -1).transpose(2, 0, 1, 3, 4)]
  transfers between devices with their start and end apart: 8 -> 22, of which waited for: 6 -> 17; matrix products, arithmetic and copies ran while one was open for 9% -> 10% of each run, Pallas kernels for 0% -> 0%
where the time goes in v4:
time: 345 us
  waiting for transfers between devices  214 us (62%)
  starting transfers between devices  39.2 us (11%)
  matrix products  37.8 us (11%)
  local copies, waits for them, and re-layouts  33.2 us (10%)
  other arithmetic  19.8 us (6%)
    ppermute x9, waiting for transfers between devices, scatter_axis(): total = total + lax.ppermute(chunk, axis, shift_pairs(n, k))  131 us
    ppermute x9, waiting for transfers between devices, gather_axis(): got = lax.ppermute(a, axis, shift_pairs(n, k))  70.7 us
    ppermute x9, starting transfers between devices, gather_axis(): got = lax.ppermute(a, axis, shift_pairs(n, k))  21.7 us
    ppermute x9, starting transfers between devices, scatter_axis(): total = total + lax.ppermute(chunk, axis, shift_pairs(n, k))  11.6 us
    add x1, local copies, waits for them, and re-layouts, local(): part = grad_mine + lax.ppermute(grad_theirs, REP, core_pairs(nrep))  9.74 us
    dot_general x2, matrix products, expert_block(): lax.dot_general(joint_grad, gate_up, (((1,), (1,)), ((), ())), preferred_...  8.91 us
    dot_general x2, matrix products, expert_block(): project = jnp.dot(inputs, gate_up, preferred_element_type=jnp.float32)  8.39 us
    ppermute x1, waiting for transfers between devices, local(): theirs = lax.ppermute(mine, REP, core_pairs(nrep))  7.56 us
  transfers between devices with their start and end apart: 22, of which 17 were waited for; matrix products, arithmetic and copies ran while one was open for 10% of the time, Pallas kernels for 0%

profile of v4, /device:TPU:1, one launch (start us, length us, event | category | flops | bytes accessed | tf_op | source)
XLA Modules:
  0.0 344.6 jit_solution(15445199684154773998)
XLA Ops:
  1.8 2.1 collective-permute-start
  3.9 2.5 collective-permute-start.1
  7.5 1.8 collective-permute-done.1
  9.9 3.4 collective-permute-start.3
  13.3 5.1 %collective-permute-start.4 = (bf16[128,1152]{1,0:T(8,128)(2,1)S(1)}, bf16[128,1152]{1,0:T(8,128)(2,1)S(1)}, u32[]{:S(2)}, u32[]{:S(2)}) collective-permute-start(bf16[128,1152]{1,0:T(8,128)(2,1)S(1)} %constant_dynamic-update-slice_fusion.8), channel_id=1, source_target_pairs={{0,32},{16,48},{32,0},{48,16},{1,33},{17,49},{33,1},{49,17},{2,34}... | collective-permute-start | bytes 884744 | tf_op jit(solution)/shard_map/ppermute | solution.py:110
  18.4 2.4 collective-permute-start.5
  20.9 2.8 collective-permute-done.3
  23.7 11.8 %collective-permute-done.4 = bf16[128,1152]{1,0:T(8,128)(2,1)S(1)} collective-permute-done((bf16[128,1152]{1,0:T(8,128)(2,1)S(1)}, bf16[128,1152]{1,0:T(8,128)(2,1)S(1)}, u32[]{:S(2)}, u32[]{:S(2)}) %collective-permute-start.4) | collective-permute-done | bytes 294944 | tf_op jit(solution)/shard_map/ppermute | solution.py:110
  35.6 9.3 %collective-permute-done.5 = bf16[128,1152]{1,0:T(8,128)(2,1)S(1)} collective-permute-done((bf16[128,1152]{1,0:T(8,128)(2,1)S(1)}, bf16[128,1152]{1,0:T(8,128)(2,1)S(1)}, u32[]{:S(2)}, u32[]{:S(2)}) %collective-permute-start.5) | collective-permute-done | bytes 294944 | tf_op jit(solution)/shard_map/ppermute | solution.py:110
  46.3 2.6 collective-permute-start.7
  50.0 2.5 broadcast_in_dim.58
  53.6 19.0 %collective-permute-done.6 = bf16[512,1152]{1,0:T(8,128)(2,1)S(1)} collective-permute-done((bf16[512,1152]{1,0:T(8,128)(2,1)S(1)}, bf16[512,1152]{1,0:T(8,128)(2,1)S(1)}, u32[]{:S(2)}, u32[]{:S(2)}) %collective-permute-start.6) | collective-permute-done | bytes 1179680 | tf_op jit(solution)/shard_map/ppermute | solution.py:110
  73.8 25.4 %collective-permute-done.7 = bf16[512,1152]{1,0:T(8,128)(2,1)} collective-permute-done((bf16[512,1152]{1,0:T(8,128)(2,1)S(1)}, bf16[512,1152]{1,0:T(8,128)(2,1)}, u32[]{:S(2)}, u32[]{:S(2)}) %collective-permute-start.7) | collective-permute-done | bytes 1179680 | tf_op jit(solution)/shard_map/ppermute | solution.py:110
  99.2 2.4 constant_dynamic-update-slice_fusion.1
  101.6 2.5 constant_dynamic-update-slice_fusion
  104.1 2.0 collective-permute-start.9
  106.4 7.6 %collective-permute-done.9 = bf16[2048,1152]{1,0:T(8,128)(2,1)} collective-permute-done((bf16[2048,1152]{1,0:T(8,128)(2,1)}, bf16[2048,1152]{1,0:T(8,128)(2,1)}, u32[]{:S(2)}, u32[]{:S(2)}) %collective-permute-start.9) | collective-permute-done | bytes 4718624 | tf_op jit(solution)/shard_map/ppermute | solution.py:73
  114.0 3.9 %fusion.1 = f32[512,768]{1,0:T(8,128)S(1)} fusion(bf16[2048,1152]{1,0:T(8,128)(2,1)} %collective-permute-done.9, bf16[512,2048]{1,0:T(8,128)(2,1)S(1)} %copy-done.3, pred[512]{0:T(512)(128)(4,1)S(1)} %get-tuple-element.10), kind=kOutput, calls=%fused_computation.7 | convolution fusion | flops 1611661312 | bytes 6816256 | tf_op jit(solution)/shard_map/dot_general | solution.py:15
  117.9 3.0 multiply_convert_fusion.1
  120.9 2.8 fusion.23
  123.7 2.0 fusion.22
  125.7 6.6 %pad_maximum_fusion = f32[2048,1152]{0,1:T(8,128)} fusion(f32[2048,384]{0,1:T(8,128)} %fusion.23, f32[2048,768]{0,1:T(8,128)S(1)} %fusion.22), kind=kLoop, calls=%fused_computation.1 | loop fusion | flops 2359296 | bytes 18874368 | tf_op jit(solution)/shard_map/concatenate | solution.py:37
  132.7 4.5 %fusion.4 = f32[512,768]{1,0:T(8,128)S(1)} fusion(bf16[2048,1152]{1,0:T(8,128)(2,1)} %constant_dynamic-update-slice_fusion, bf16[512,2048]{1,0:T(8,128)(2,1)} %param.4, pred[512]{0:T(512)(128)(4,1)S(1)} %get-tuple-element.9), kind=kOutput, calls=%fused_computation.10 | convolution fusion | flops 1611661312 | bytes 6816256 | tf_op jit(solution)/shard_map/dot_general | solution.py:15
  137.2 3.0 multiply_convert_fusion.3
  142.2 2.0 fusion.20
  144.2 3.1 collective-permute-done.10
  147.3 7.1 %maximum_add_fusion = f32[2048,1152]{0,1:T(8,128)} fusion(f32[2048,1152]{0,1:T(8,128)} %collective-permute-done.10, f32[2048,384]{0,1:T(8,128)S(1)} %fusion.21, f32[2048,768]{0,1:T(8,128)S(1)} %fusion.20), kind=kLoop, calls=%fused_computation | loop fusion | flops 4718592 | bytes 28311552 | tf_op jit(solution)/shard_map/add | solution.py:86
  154.4 9.7 %copy.25 = f32[2048,1152]{1,0:T(8,128)} copy(f32[2048,1152]{0,1:T(8,128)} %maximum_add_fusion) | data formatting | bytes 18874368 | tf_op jit(solution)/shard_map/add | solution.py:86
  164.1 4.3 %copy.26 = f32[4,4,4,32,1152]{4,3,2,1,0:T(8,128)S(1)} copy(f32[4,4,4,32,1152]{4,3,0,2,1:T(8,128)} %bitcast.21) | data formatting | bytes 18874368 | tf_op jit(solution)/shard_map/transpose | solution.py:87
  168.4 3.0 constant_dynamic-slice_fusion.8
  171.4 2.0 copy-done.2
  173.4 2.1 collective-permute-start.13
  176.1 50.4 %collective-permute-done.13 = f32[512,1152]{1,0:T(8,128)} collective-permute-done((f32[512,1152]{1,0:T(8,128)}, f32[512,1152]{1,0:T(8,128)}, u32[]{:S(2)}, u32[]{:S(2)}) %collective-permute-start.13) | collective-permute-done | bytes 2359328 | tf_op jit(solution)/shard_map/ppermute | solution.py:122
  226.5 3.1 collective-permute-done.12
  229.6 50.5 %collective-permute-done.11 = f32[512,1152]{1,0:T(8,128)} collective-permute-done((f32[512,1152]{1,0:T(8,128)S(1)}, f32[512,1152]{1,0:T(8,128)}, u32[]{:S(2)}, u32[]{:S(2)}) %collective-permute-start.11) | collective-permute-done | bytes 2359328 | tf_op jit(solution)/shard_map/ppermute | solution.py:122
  280.1 4.2 %add_add_fusion = f32[512,1152]{1,0:T(8,128)S(1)} fusion(f32[512,1152]{1,0:T(8,128)} %collective-permute-done.13, f32[512,1152]{1,0:T(8,128)} %collective-permute-done.12, f32[512,1152]{1,0:T(8,128)} %collective-permute-done.11, f32[2048,1152]{1,0:T(8,128)} %bitcast.20, s32[]{:T(128)S(6)} %select_n.250), kind=kLoop, calls=%fused_computation.14 | loop fusion | flops 1769472 | bytes 11796484 | tf_op jit(solution)/shard_map/add | solution.py:122
  285.4 1.6 collective-permute-start.15
  287.9 3.9 %fusion.11 = bf16[512,2048]{1,0:T(8,128)(2,1)S(1)} fusion(bf16[2048,1152]{1,0:T(8,128)(2,1)} %collective-permute-done.9, pred[512]{0:T(512)(128)(4,1)S(1)} %get-tuple-element.10, bf16[512,384]{1,0:T(8,128)(2,1)} %copy-done.8, bf16[512,384]{1,0:T(8,128)(2,1)S(1)} %copy-done.7), kind=kOutput, calls=%fused_computation.16 | convolution fusion | flops 1614282752 | bytes 6029824 | tf_op jit(solution)/shard_map/dot_general | solution.py:34
  291.8 7.7 %collective-permute-done.16 = f32[128,1152]{1,0:T(8,128)} collective-permute-done((f32[128,1152]{1,0:T(8,128)}, f32[128,1152]{1,0:T(8,128)}, u32[]{:S(2)}, u32[]{:S(2)}) %collective-permute-start.16) | collective-permute-done | bytes 589856 | tf_op jit(solution)/shard_map/ppermute | solution.py:122
  299.5 1.6 collective-permute-done.15
  301.1 14.0 %collective-permute-done.14 = f32[128,1152]{1,0:T(8,128)} collective-permute-done((f32[128,1152]{1,0:T(8,128)S(1)}, f32[128,1152]{1,0:T(8,128)}, u32[]{:S(2)}, u32[]{:S(2)}) %collective-permute-start.14) | collective-permute-done | bytes 589856 | tf_op jit(solution)/shard_map/ppermute | solution.py:122
  316.7 3.3 collective-permute-start.19
  321.3 1.7 collective-permute-start.17
  323.1 5.1 %fusion.8 = bf16[512,2048]{1,0:T(8,128)(2,1)} fusion(bf16[512,2048]{1,0:T(8,128)(2,1)S(1)} %fusion.11, bf16[2048,1152]{1,0:T(8,128)(2,1)} %constant_dynamic-update-slice_fusion, pred[512]{0:T(512)(128)(4,1)S(1)} %get-tuple-element.9, bf16[512,384]{1,0:T(8,128)(2,1)S(1)} %copy-done.12, bf16[512,384]{1,0:T(8,128)(2,1)S(1)} %copy-done.10), kind=kOutput, calls=%fused_computation.15 | convolution fusion | flops 1614282752 | bytes 8126976 | tf_op jit(solution)/shard_map/dot_general | solution.py:34
  328.1 3.7 %collective-permute-done.18 = f32[32,1152]{1,0:T(8,128)S(1)} collective-permute-done((f32[32,1152]{1,0:T(8,128)S(1)}, f32[32,1152]{1,0:T(8,128)S(1)}, u32[]{:S(2)}, u32[]{:S(2)}) %collective-permute-start.18) | collective-permute-done | bytes 147488 | tf_op jit(solution)/shard_map/ppermute | solution.py:122
  332.1 2.7 fusion.7
  336.0 3.5 %collective-permute-start.21 = (f32[32,1152]{1,0:T(8,128)S(1)}, f32[32,1152]{1,0:T(8,128)S(1)}, u32[]{:S(2)}, u32[]{:S(2)}) collective-permute-start(f32[32,1152]{1,0:T(8,128)S(1)} %add.309), channel_id=1, source_target_pairs={{0,1},{1,0},{2,3},{3,2},{4,5},{5,4},{6,7},{7,6},{8,9},{9,8},{10,11... | collective-permute-start | bytes 442376 | tf_op jit(solution)/shard_map/ppermute | solution.py:92
  339.6 4.1 %fusion.6 = bf16[512,2048]{1,0:T(8,128)(2,1)} fusion(bf16[512,2048]{1,0:T(8,128)(2,1)S(1)} %fusion.7, bf16[512,384]{1,0:T(8,128)(2,1)S(1)} %copy-done.19, pred[512]{0:T(512)(128)(4,1)S(1)} %get-tuple-element.9, bf16[2048,1152]{1,0:T(8,128)(2,1)} %constant_dynamic-update-slice_fusion), kind=kOutput, calls=%fused_computation.12 | convolution fusion | flops 807403520 | bytes 6160896 | tf_op jit(solution)/shard_map/dot_general | solution.py:21
  (83 shorter events, 18.4 us)
Async XLA Ops:
  0.6 0.9 copy-start
  1.8 5.7 %collective-permute-start = (bf16[32,1152]{1,0:T(8,128)(2,1)S(1)}, bf16[32,1152]{1,0:T(8,128)(2,1)S(1)}, u32[]{:S(2)}, u32[]{:S(2)}) collective-permute-start(bf16[32,1152]{1,0:T(8,128)(2,1)S(1)} %get-tuple-element.12), channel_id=1, source_target_pairs={{0,4},{4,8},{8,12},{12,0},{1,5},{5,9},{9,13},{13,1},{2,6},{6,10},{... | collective-permute-start | bytes 221192 | tf_op jit(solution)/shard_map/ppermute | solution.py:110
  3.9 5.4 %collective-permute-start.1 = (bf16[32,1152]{1,0:T(8,128)(2,1)S(1)}, bf16[32,1152]{1,0:T(8,128)(2,1)S(1)}, u32[]{:S(2)}, u32[]{:S(2)}) collective-permute-start(bf16[32,1152]{1,0:T(8,128)(2,1)S(1)} %get-tuple-element.12), channel_id=1, source_target_pairs={{0,8},{4,12},{8,0},{12,4},{1,9},{5,13},{9,1},{13,5},{2,10},{6,14},... | collective-permute-start | bytes 221192 | tf_op jit(solution)/shard_map/ppermute | solution.py:110
  6.3 3.5 %collective-permute-start.2 = (bf16[32,1152]{1,0:T(8,128)(2,1)S(1)}, bf16[32,1152]{1,0:T(8,128)(2,1)S(1)}, u32[]{:S(2)}, u32[]{:S(2)}) collective-permute-start(bf16[32,1152]{1,0:T(8,128)(2,1)S(1)} %get-tuple-element.12), channel_id=1, source_target_pairs={{0,12},{4,0},{8,4},{12,8},{1,13},{5,1},{9,5},{13,9},{2,14},{6,2},{... | collective-permute-start | bytes 221192 | tf_op jit(solution)/shard_map/ppermute | solution.py:110
  9.9 13.8 %collective-permute-start.3 = (bf16[128,1152]{1,0:T(8,128)(2,1)S(1)}, bf16[128,1152]{1,0:T(8,128)(2,1)S(1)}, u32[]{:S(2)}, u32[]{:S(2)}) collective-permute-start(bf16[128,1152]{1,0:T(8,128)(2,1)S(1)} %constant_dynamic-update-slice_fusion.8), channel_id=1, source_target_pairs={{0,16},{16,32},{32,48},{48,0},{1,17},{17,33},{33,49},{49,1},{2,18}... | collective-permute-start | bytes 884744 | tf_op jit(solution)/shard_map/ppermute | solution.py:110
  13.3 22.3 %collective-permute-start.4 = (bf16[128,1152]{1,0:T(8,128)(2,1)S(1)}, bf16[128,1152]{1,0:T(8,128)(2,1)S(1)}, u32[]{:S(2)}, u32[]{:S(2)}) collective-permute-start(bf16[128,1152]{1,0:T(8,128)(2,1)S(1)} %constant_dynamic-update-slice_fusion.8), channel_id=1, source_target_pairs={{0,32},{16,48},{32,0},{48,16},{1,33},{17,49},{33,1},{49,17},{2,34}... | collective-permute-start | bytes 884744 | tf_op jit(solution)/shard_map/ppermute | solution.py:110
  18.4 26.5 %collective-permute-start.5 = (bf16[128,1152]{1,0:T(8,128)(2,1)S(1)}, bf16[128,1152]{1,0:T(8,128)(2,1)S(1)}, u32[]{:S(2)}, u32[]{:S(2)}) collective-permute-start(bf16[128,1152]{1,0:T(8,128)(2,1)S(1)} %constant_dynamic-update-slice_fusion.8), channel_id=1, source_target_pairs={{0,48},{16,0},{32,16},{48,32},{1,49},{17,1},{33,17},{49,33},{2,50}... | collective-permute-start | bytes 884744 | tf_op jit(solution)/shard_map/ppermute | solution.py:110
  44.9 27.8 %collective-permute-start.6 = (bf16[512,1152]{1,0:T(8,128)(2,1)S(1)}, bf16[512,1152]{1,0:T(8,128)(2,1)S(1)}, u32[]{:S(2)}, u32[]{:S(2)}) collective-permute-start(bf16[512,1152]{1,0:T(8,128)(2,1)S(1)} %constant_dynamic-update-slice_fusion.4), channel_id=1, source_target_pairs={{0,64},{64,128},{128,192},{192,0},{1,65},{65,129},{129,193},{193,1... | collective-permute-start | bytes 3538952 | tf_op jit(solution)/shard_map/ppermute | solution.py:110
  46.3 52.9 %collective-permute-start.7 = (bf16[512,1152]{1,0:T(8,128)(2,1)S(1)}, bf16[512,1152]{1,0:T(8,128)(2,1)}, u32[]{:S(2)}, u32[]{:S(2)}) collective-permute-start(bf16[512,1152]{1,0:T(8,128)(2,1)S(1)} %constant_dynamic-update-slice_fusion.4), channel_id=1, source_target_pairs={{0,128},{64,192},{128,0},{192,64},{1,129},{65,193},{129,1},{193,65... | collective-permute-start | bytes 3538952 | tf_op jit(solution)/shard_map/ppermute | solution.py:110
  48.9 52.7 %collective-permute-start.8 = (bf16[512,1152]{1,0:T(8,128)(2,1)S(1)}, bf16[512,1152]{1,0:T(8,128)(2,1)}, u32[]{:S(2)}, u32[]{:S(2)}) collective-permute-start(bf16[512,1152]{1,0:T(8,128)(2,1)S(1)} %constant_dynamic-update-slice_fusion.4), channel_id=1, source_target_pairs={{0,192},{64,0},{128,64},{192,128},{1,193},{65,1},{129,65},{193,129... | collective-permute-start | bytes 3538952 | tf_op jit(solution)/shard_map/ppermute | solution.py:110
  73.8 32.3 %copy-start.13 = (s32[1,2]{1,0:T(1,128)S(1)}, s32[1,2]{1,0:T(1,128)}, u32[]{:S(2)}) copy-start(s32[1,2]{1,0:T(1,128)} %param.6) | copy-start | bytes 28
  73.8 40.2 %copy-start.3 = (bf16[512,2048]{1,0:T(8,128)(2,1)S(1)}, bf16[512,2048]{1,0:T(8,128)(2,1)}, u32[]{:S(2)}) copy-start(bf16[512,2048]{1,0:T(8,128)(2,1)} %param.4) | copy-start | bytes 6291460
  104.1 9.9 %collective-permute-start.9 = (bf16[2048,1152]{1,0:T(8,128)(2,1)}, bf16[2048,1152]{1,0:T(8,128)(2,1)}, u32[]{:S(2)}, u32[]{:S(2)}) collective-permute-start(bf16[2048,1152]{1,0:T(8,128)(2,1)} %constant_dynamic-update-slice_fusion), channel_id=1, source_target_pairs={{0,1},{1,0},{2,3},{3,2},{4,5},{5,4},{6,7},{7,6},{8,9},{9,8},{10,11... | collective-permute-start | bytes 14155784 | tf_op jit(solution)/shard_map/ppermute | solution.py:73
  114.0 3.9 %copy-start.14 = (bf16[512,2048]{1,0:T(8,128)(2,1)S(1)}, bf16[512,2048]{1,0:T(8,128)(2,1)}, u32[]{:S(2)}) copy-start(bf16[512,2048]{1,0:T(8,128)(2,1)} %param.5) | copy-start | bytes 6291460
  120.9 2.8 copy-start.16
  120.9 2.8 copy-start.6
  120.9 2.8 copy-start.8
  120.9 2.8 copy-start.4
  132.3 15.0 %collective-permute-start.10 = (f32[2048,1152]{0,1:T(8,128)}, f32[2048,1152]{0,1:T(8,128)}, u32[]{:S(2)}, u32[]{:S(2)}) collective-permute-start(f32[2048,1152]{0,1:T(8,128)} %pad_maximum_fusion), channel_id=1, source_target_pairs={{0,1},{1,0},{2,3},{3,2},{4,5},{5,4},{6,7},{7,6},{8,9},{9,8},{10,11... | collective-permute-start | bytes 28311560 | tf_op jit(solution)/shard_map/ppermute | solution.py:86
  132.7 4.5 %copy-start.15 = (bf16[512,2048]{1,0:T(8,128)(2,1)S(1)}, bf16[512,2048]{1,0:T(8,128)(2,1)}, u32[]{:S(2)}) copy-start(bf16[512,2048]{1,0:T(8,128)(2,1)} %param.5) | copy-start | bytes 6291460
  140.1 1.1 copy-start.18
  140.2 1.1 copy-start.9
  140.2 1.1 copy-start.11
  140.2 2.0 copy-start.5
  168.4 5.0 %copy-start.2 = (f32[4,4,4,32,1152]{4,3,2,1,0:T(8,128)}, f32[4,4,4,32,1152]{4,3,2,1,0:T(8,128)S(1)}, u32[]{:S(2)}) copy-start(f32[4,4,4,32,1152]{4,3,2,1,0:T(8,128)S(1)} %copy.26) | copy-start | bytes 28311556
  173.4 53.1 %collective-permute-start.13 = (f32[512,1152]{1,0:T(8,128)}, f32[512,1152]{1,0:T(8,128)}, u32[]{:S(2)}, u32[]{:S(2)}) collective-permute-start(f32[512,1152]{1,0:T(8,128)} %get-tuple-element.14), channel_id=1, source_target_pairs={{0,12},{4,0},{8,4},{12,8},{1,13},{5,1},{9,5},{13,9},{2,14},{6,2},{... | collective-permute-start | bytes 7077896 | tf_op jit(solution)/shard_map/ppermute | solution.py:122
  175.5 54.1 %collective-permute-start.12 = (f32[512,1152]{1,0:T(8,128)}, f32[512,1152]{1,0:T(8,128)}, u32[]{:S(2)}, u32[]{:S(2)}) collective-permute-start(f32[512,1152]{1,0:T(8,128)} %get-tuple-element.15), channel_id=1, source_target_pairs={{0,8},{4,12},{8,0},{12,4},{1,9},{5,13},{9,1},{13,5},{2,10},{6,14},... | collective-permute-start | bytes 7077896 | tf_op jit(solution)/shard_map/ppermute | solution.py:122
  175.5 104.5 %collective-permute-start.11 = (f32[512,1152]{1,0:T(8,128)S(1)}, f32[512,1152]{1,0:T(8,128)}, u32[]{:S(2)}, u32[]{:S(2)}) collective-permute-start(f32[512,1152]{1,0:T(8,128)S(1)} %get-tuple-element.13), channel_id=1, source_target_pairs={{0,4},{4,8},{8,12},{12,0},{1,5},{5,9},{9,13},{13,1},{2,6},{6,10},{... | collective-permute-start | bytes 7077896 | tf_op jit(solution)/shard_map/ppermute | solution.py:122
  284.2 3.7 %copy-start.7 = (bf16[512,384]{1,0:T(8,128)(2,1)S(1)}, bf16[512,384]{1,0:T(8,128)(2,1)}, u32[]{:S(2)}) copy-start(bf16[512,384]{1,0:T(8,128)(2,1)} %copy-done.6) | copy-start | bytes 1179652
  285.4 14.1 %collective-permute-start.16 = (f32[128,1152]{1,0:T(8,128)}, f32[128,1152]{1,0:T(8,128)}, u32[]{:S(2)}, u32[]{:S(2)}) collective-permute-start(f32[128,1152]{1,0:T(8,128)} %get-tuple-element.17), channel_id=1, source_target_pairs={{0,192},{64,0},{128,64},{192,128},{1,193},{65,1},{129,65},{193,129... | collective-permute-start | bytes 1769480 | tf_op jit(solution)/shard_map/ppermute | solution.py:122
  285.4 15.7 %collective-permute-start.15 = (f32[128,1152]{1,0:T(8,128)}, f32[128,1152]{1,0:T(8,128)}, u32[]{:S(2)}, u32[]{:S(2)}) collective-permute-start(f32[128,1152]{1,0:T(8,128)} %get-tuple-element.18), channel_id=1, source_target_pairs={{0,128},{64,192},{128,0},{192,64},{1,129},{65,193},{129,1},{193,65... | collective-permute-start | bytes 1769480 | tf_op jit(solution)/shard_map/ppermute | solution.py:122
  287.0 28.1 %collective-permute-start.14 = (f32[128,1152]{1,0:T(8,128)S(1)}, f32[128,1152]{1,0:T(8,128)}, u32[]{:S(2)}, u32[]{:S(2)}) collective-permute-start(f32[128,1152]{1,0:T(8,128)S(1)} %get-tuple-element.16), channel_id=1, source_target_pairs={{0,64},{64,128},{128,192},{192,0},{1,65},{65,129},{129,193},{193,1... | collective-permute-start | bytes 1769480 | tf_op jit(solution)/shard_map/ppermute | solution.py:122
  291.8 31.3 %copy-start.10 = (bf16[512,384]{1,0:T(8,128)(2,1)S(1)}, bf16[512,384]{1,0:T(8,128)(2,1)}, u32[]{:S(2)}) copy-start(bf16[512,384]{1,0:T(8,128)(2,1)} %copy-done.9) | copy-start | bytes 1179652
  291.8 31.3 %copy-start.12 = (bf16[512,384]{1,0:T(8,128)(2,1)S(1)}, bf16[512,384]{1,0:T(8,128)(2,1)}, u32[]{:S(2)}) copy-start(bf16[512,384]{1,0:T(8,128)(2,1)} %copy-done.11) | copy-start | bytes 1179652
  316.7 11.5 %collective-permute-start.19 = (f32[32,1152]{1,0:T(8,128)S(1)}, f32[32,1152]{1,0:T(8,128)S(1)}, u32[]{:S(2)}, u32[]{:S(2)}) collective-permute-start(f32[32,1152]{1,0:T(8,128)S(1)} %get-tuple-element.26), channel_id=1, source_target_pairs={{0,48},{16,0},{32,16},{48,32},{1,49},{17,1},{33,17},{49,33},{2,50}... | collective-permute-start | bytes 442376 | tf_op jit(solution)/shard_map/ppermute | solution.py:122
  320.0 11.9 %collective-permute-start.18 = (f32[32,1152]{1,0:T(8,128)S(1)}, f32[32,1152]{1,0:T(8,128)S(1)}, u32[]{:S(2)}, u32[]{:S(2)}) collective-permute-start(f32[32,1152]{1,0:T(8,128)S(1)} %get-tuple-element.27), channel_id=1, source_target_pairs={{0,32},{16,48},{32,0},{48,16},{1,33},{17,49},{33,1},{49,17},{2,34}... | collective-permute-start | bytes 442376 | tf_op jit(solution)/shard_map/ppermute | solution.py:122
  321.3 10.7 %copy-start.17 = (bf16[512,384]{1,0:T(8,128)(2,1)S(1)}, bf16[512,384]{1,0:T(8,128)(2,1)}, u32[]{:S(2)}) copy-start(bf16[512,384]{1,0:T(8,128)(2,1)} %copy-done.16) | copy-start | bytes 1179652
  321.3 10.6 %collective-permute-start.17 = (f32[32,1152]{1,0:T(8,128)S(1)}, f32[32,1152]{1,0:T(8,128)S(1)}, u32[]{:S(2)}, u32[]{:S(2)}) collective-permute-start(f32[32,1152]{1,0:T(8,128)S(1)} %get-tuple-element.25), channel_id=1, source_target_pairs={{0,16},{16,32},{32,48},{48,0},{1,17},{17,33},{33,49},{49,1},{2,18}... | collective-permute-start | bytes 442376 | tf_op jit(solution)/shard_map/ppermute | solution.py:122
  331.9 7.6 %copy-start.19 = (bf16[512,384]{1,0:T(8,128)(2,1)S(1)}, bf16[512,384]{1,0:T(8,128)(2,1)}, u32[]{:S(2)}) copy-start(bf16[512,384]{1,0:T(8,128)(2,1)} %copy-done.18) | copy-start | bytes 1179652
  331.9 4.1 %collective-permute-start.20 = (f32[32,1152]{1,0:T(8,128)S(1)}, f32[32,1152]{1,0:T(8,128)S(1)}, u32[]{:S(2)}, u32[]{:S(2)}) collective-permute-start(f32[32,1152]{1,0:T(8,128)S(1)} %add_add_fusion.2), channel_id=1, source_target_pairs={{0,2},{1,3},{2,0},{3,1},{4,6},{5,7},{6,4},{7,5},{8,10},{9,11},{10,... | collective-permute-start | bytes 442376 | tf_op jit(solution)/shard_map/ppermute | solution.py:91
  336.0 7.6 %collective-permute-start.21 = (f32[32,1152]{1,0:T(8,128)S(1)}, f32[32,1152]{1,0:T(8,128)S(1)}, u32[]{:S(2)}, u32[]{:S(2)}) collective-permute-start(f32[32,1152]{1,0:T(8,128)S(1)} %add.309), channel_id=1, source_target_pairs={{0,1},{1,0},{2,3},{3,2},{4,5},{5,4},{6,7},{7,6},{8,9},{9,8},{10,11... | collective-permute-start | bytes 442376 | tf_op jit(solution)/shard_map/ppermute | solution.py:92
  339.6 5.1 %copy-start.1 = (bf16[32,2,1152]{2,1,0:T(2,128)(2,1)S(1)}, bf16[32,2,1152]{2,1,0:T(2,128)(2,1)}, u32[]{:S(2)}) copy-start(bf16[32,2,1152]{2,1,0:T(2,128)(2,1)} %param.7) | copy-start | bytes 442372
